TPU v7x, 128 devices: a whole 4x4x4 slice. The times are simulated.
128 devices in a mesh: seq: 16 (over x_hi, z, core), tp: 8 (over y, x_lo).
Axes of the slice: x: 4 (x_hi: 2, x_lo: 2; x = x_hi * 2 + x_lo), y: 4, z: 4, core: 2. Of those that a mesh axis runs over, the one named last changes fastest.
Arguments:
- tokens: bfloat16 [4, 2048, 4096], P(None, 'seq', 'tp'), may hold values from -6 to 6
- new_tokens: bfloat16 [4, 4096], P(None, 'tp'), may hold values from -6 to 6
- w_qkv: bfloat16 [3, 4096, 4096], P(None, None, 'tp')
- w_out: bfloat16 [4096, 4096], P('tp')
- q_gain: float32 [4096], P('tp'), may hold values from 0.5 to 6
- k_gain: float32 [4096], P('tp'), may hold values from 0.5 to 6
- post_gain: float32 [4096], P('tp'), may hold values from 0.5 to 1.5
- lengths: int32 [4], replicated, may hold values from 1 to 2048, 6144 in all
Outputs:
- hidden_out: bfloat16 [4, 2048, 4096], P(None, 'seq', 'tp')
- new_out: bfloat16 [4, 4096], P(None, 'tp')
Inputs may be any that keep to these rules, and one draw needn't show every extreme that they name: `lengths`: one prompt has exactly 2048 live tokens.
All inputs are finite; a program needn't handle non-finite values.
Results may differ from a plain program's by a relative error of at most 0.012.
The roundings to bfloat16 on the way count: a program that leaves them out, or rounds other values in their place, can miss the bound.
Values may be sent and summed in bfloat16 or wider, within the bound.
No kernel may reach another device: no remote copies, remote signals or barrier semaphores. Data moves between devices by JAX's collectives and lax.ppermute only.
A program may use at most 128 MiB of HBM per device.

v0:
```python
import jax
import jax.numpy as jnp
from jax import lax
from jax.experimental import pallas as pl
from jax.experimental.pallas import tpu as pltpu
from jax.sharding import PartitionSpec as P

HD = 128


rope_base = 500000.0
norm_eps = 1e-06
masked_fill = -1e30


def rotate(values, position):
    half = values.shape[-1] // 2
    freq = rope_base ** (-(jnp.arange(half, dtype=jnp.float32) * 2.0) / values.shape[-1])
    angle = position.astype(jnp.float32)[..., None] * freq
    cosine = jnp.cos(angle)
    sine = jnp.sin(angle)
    lower = values[..., :half]
    upper = values[..., half:]
    return jnp.concatenate([lower * cosine - upper * sine, upper * cosine + lower * sine], -1)


RELATIVE = ("own", "ax", "aup", "adn", "m1", "m2", "m3", "m4")


def tp_links(width):
    size = 8
    cross = [(i, i ^ 1) for i in range(size)]
    up = [(i, (i + 2) % size) for i in range(size)]
    down = [(i, (i - 2) % size) for i in range(size)]
    t = lax.axis_index("tp")
    y, x = t // 2, t % 2
    other = 1 - x

    def block(dy, side):
        return ((y + dy) % 4) * 2 + side

    order = {
        "own": block(0, x), "ax": block(0, other), "aup": block(-1, x), "adn": block(1, x),
        "m1": block(1, other), "m2": block(-1, other), "m3": block(2, x), "m4": block(2, other),
    }
    return cross, up, down, order


def tp_gather(piece):
    width = piece.shape[1]
    half, quarter = width // 2, width // 4
    cross, up, down, order = tp_links(width)
    send = lambda value, perm: lax.ppermute(value, "tp", perm)
    ax = send(piece, cross)
    aup = send(piece, up)
    adn = send(piece, down)
    bx = send(jnp.concatenate([adn[:, :half], aup[:, :half]], 1), cross)
    bdn = send(jnp.concatenate([ax[:, half:], adn[:, :half]], 1), down)
    bup = send(jnp.concatenate([ax[:, half:], aup[:, half:]], 1), up)
    m1 = jnp.concatenate([bx[:, :half], bdn[:, :half]], 1)
    m2 = jnp.concatenate([bx[:, half:], bup[:, :half]], 1)
    m3 = jnp.concatenate([bdn[:, half:], bup[:, half:]], 1)
    cx = send(m3[:, :half], cross)
    cdn = send(m1[:, half:half + quarter], down)
    cup = send(m2[:, half + quarter:], up)
    m4 = jnp.concatenate([cx, cdn, cup], 1)
    return [[piece, ax, aup, adn], [m1, m2, m3], [m4]], order


def tp_reduce_scatter(b, width):
    half, quarter = width // 2, width // 4
    cross, up, down, order = tp_links(width)
    send = lambda value, perm: lax.ppermute(value.astype(jnp.bfloat16), "tp", perm).astype(jnp.float32)
    rx = send(b["m4"][:, :half], cross)
    rup = send(b["m4"][:, half:half + quarter], up)
    rdn = send(b["m4"][:, half + quarter:], down)
    m1, m2, m3 = b["m1"], b["m2"], b["m3"]
    m3 = jnp.concatenate([m3[:, :half] + rx, m3[:, half:]], 1)
    m1 = jnp.concatenate([m1[:, :half], m1[:, half:half + quarter] + rup, m1[:, half + quarter:]], 1)
    m2 = jnp.concatenate([m2[:, :half + quarter], m2[:, half + quarter:] + rdn], 1)
    rx = send(jnp.concatenate([m1[:, :half], m2[:, :half]], 1), cross)
    rup = send(jnp.concatenate([m1[:, half:], m3[:, :half]], 1), up)
    rdn = send(jnp.concatenate([m2[:, half:], m3[:, half:]], 1), down)
    ax = jnp.concatenate([b["ax"][:, :half], b["ax"][:, half:] + rup[:, :half] + rdn[:, :half]], 1)
    adn = jnp.concatenate([b["adn"][:, :half] + rx[:, :half] + rup[:, half:], b["adn"][:, half:]], 1)
    aup = jnp.concatenate([b["aup"][:, :half] + rx[:, half:], b["aup"][:, half:] + rdn[:, half:]], 1)
    return b["own"] + send(ax, cross) + send(adn, up) + send(aup, down)


def tp_sum(values):
    for bit in (1, 2, 4):
        values = jax.tree.map(
            lambda v, bit=bit: v + lax.ppermute(v, "tp", [(i, i ^ bit) for i in range(8)]), values
        )
    return values


def rope_pack(proj, square, gains, cosine, sine, seqs, pos_dev, full_width):
    _, rows, width = proj.shape
    heads = width // HD

    def kernel(proj_ref, square_ref, gain_ref, cos_ref, sin_ref, pack_ref, fresh_ref):
        cos_v = cos_ref[...]
        sin_v = sin_ref[...]
        for c in range(3):
            x = proj_ref[c]
            if c < 2:
                x = x * lax.rsqrt(square_ref[c] / full_width + norm_eps) * gain_ref[c]
            for h in range(heads):
                xh = x[:, h * HD:(h + 1) * HD]
                if c < 2:
                    xh = xh * cos_v + pltpu.roll(xh, HD // 2, 1) * sin_v
                xh = xh.astype(jnp.bfloat16)
                for b in range(seqs):
                    pack_ref[b * heads + h, c] = xh[b * pos_dev:(b + 1) * pos_dev]
                fresh_ref[c, :, h * HD:(h + 1) * HD] = xh[seqs * pos_dev:].astype(jnp.float32)

    return pl.pallas_call(
        kernel,
        out_shape=(
            jax.ShapeDtypeStruct((seqs * heads, 3, pos_dev, HD), jnp.bfloat16),
            jax.ShapeDtypeStruct((3, rows - seqs * pos_dev, width), jnp.float32),
        ),
    )(proj, square, gains, cosine, sine)


def attend_pair(q_all, k_all, v_all, q_new, k_new, v_new, length):
    count = q_all.shape[0]
    scale = HD ** (-0.5)
    chunks = 2
    size = count // chunks
    outs = []
    for c in range(chunks):
        stop = (c + 1) * size
        scores = (
            jnp.dot(q_all[c * size:stop], k_all[:stop].T, preferred_element_type=jnp.float32)
            * scale
        )
        query_pos = c * size + jnp.arange(size, dtype=jnp.int32)[:, None]
        key_pos = jnp.arange(stop, dtype=jnp.int32)[None, :]
        valid = (key_pos <= query_pos) & (key_pos < length)
        scores = jnp.where(valid, scores, masked_fill)
        top = jnp.max(scores, -1, keepdims=True)
        weights = jnp.where(valid, jnp.exp(scores - top), 0.0)
        total = jnp.sum(weights, -1, keepdims=True)
        outs.append(
            jnp.dot(weights.astype(jnp.bfloat16), v_all[:stop], preferred_element_type=jnp.float32)
            / total
        )
    prompt_out = jnp.concatenate(outs, 0).astype(jnp.bfloat16)
    new_scores = jnp.dot(k_all, q_new, preferred_element_type=jnp.float32) * scale
    live = jnp.arange(count, dtype=jnp.int32) < length
    new_scores = jnp.where(live, new_scores, masked_fill)
    self_score = jnp.dot(q_new, k_new, preferred_element_type=jnp.float32) * scale
    new_top = jnp.maximum(jnp.max(new_scores), self_score)
    new_weights = jnp.where(live, jnp.exp(new_scores - new_top), 0.0)
    own_weight = jnp.exp(self_score - new_top)
    new_total = jnp.sum(new_weights) + own_weight
    own_rounded = lax.optimization_barrier(own_weight.astype(jnp.bfloat16)).astype(jnp.float32)
    numer = jnp.dot(new_weights.astype(jnp.bfloat16), v_all, preferred_element_type=jnp.float32)
    numer = numer + own_rounded * v_new.astype(jnp.float32)
    return prompt_out, (numer / new_total).astype(jnp.bfloat16)


def body(tokens, new_tokens, w_qkv, w_out, q_gain, k_gain, post_gain, lengths):
    seqs, pos_dev, width_local = tokens.shape
    heads_local = width_local // HD
    full_width = w_qkv.shape[1]
    n_seq = lax.axis_size("seq")
    pairs = seqs * heads_local
    assert pairs == n_seq
    prompt_rows = seqs * pos_dev
    full_len = pos_dev * n_seq
    flat_rows = tokens.reshape(prompt_rows, width_local)
    local_rows = jnp.concatenate([flat_rows, new_tokens], 0)
    rounds, order = tp_gather(local_rows)

    def in_relative_order(weight, axis):
        return [
            lax.dynamic_slice_in_dim(weight, order[name] * width_local, width_local, axis)
            for name in RELATIVE
        ]

    w_blocks = in_relative_order(w_qkv, 1)
    proj, start = None, 0
    for blocks in rounds:
        stop = start + len(blocks)
        term = jnp.einsum(
            "tn,cnf->ctf",
            jnp.concatenate(blocks, 1),
            jnp.concatenate(w_blocks[start:stop], 1),
            preferred_element_type=jnp.float32,
        )
        proj = term if proj is None else proj + term
        start = stop
    query_raw, key_raw = proj[0], proj[1]
    query_sq, key_sq = tp_sum((jnp.sum(query_raw * query_raw, -1), jnp.sum(key_raw * key_raw, -1)))

    seq_index = lax.axis_index("seq")
    query_pos = seq_index * pos_dev + jnp.arange(pos_dev, dtype=jnp.int32)
    row_pos = jnp.concatenate([jnp.tile(query_pos, seqs), lengths.astype(jnp.int32)], 0)
    half = HD // 2
    freq = rope_base ** (-(jnp.arange(half, dtype=jnp.float32) * 2.0) / HD)
    angle = row_pos.astype(jnp.float32)[:, None] * freq
    cosine, sine = jnp.cos(angle), jnp.sin(angle)
    qkv, fresh = rope_pack(
        proj,
        jnp.stack([query_sq, key_sq])[:, :, None],
        jnp.stack([q_gain, k_gain])[:, None, :],
        jnp.concatenate([cosine, cosine], 1),
        jnp.concatenate([-sine, sine], 1),
        seqs,
        pos_dev,
        full_width,
    )

    got = lax.all_to_all(qkv, "seq", 0, 0, tiled=True)
    full = got.transpose(1, 0, 2, 3).reshape(3, full_len, HD)

    owner = seq_index
    own_prompt = owner // heads_local
    fresh = fresh.astype(jnp.bfloat16).reshape(3, pairs, HD)
    new_q, new_k, new_v = fresh[0, owner], fresh[1, owner], fresh[2, owner]
    prompt_out, new_out = attend_pair(
        full[0], full[1], full[2], new_q, new_k, new_v, lengths[own_prompt]
    )

    pad = 8
    back = jnp.concatenate(
        [prompt_out.reshape(n_seq, pos_dev, HD), jnp.broadcast_to(new_out, (n_seq, pad, HD))], 1
    )
    ret = lax.all_to_all(back, "seq", 0, 0, tiled=True)
    ret = ret.reshape(seqs, heads_local, pos_dev + pad, HD)
    attn_rows = ret[:, :, :pos_dev].transpose(0, 2, 1, 3).reshape(prompt_rows, width_local)
    attn_new = ret[:, :, pos_dev].reshape(seqs, width_local)
    attention = jnp.concatenate([attn_rows, attn_new], 0)

    wo_blocks = in_relative_order(w_out, 1)
    part = {}
    for names in (RELATIVE[7:], RELATIVE[4:7], RELATIVE[:4]):
        columns = [wo_blocks[RELATIVE.index(name)] for name in names]
        value = jnp.dot(attention, jnp.concatenate(columns, 1), preferred_element_type=jnp.float32)
        for i, name in enumerate(names):
            part[name] = value[:, i * width_local:(i + 1) * width_local]
    summed = tp_reduce_scatter(part, width_local)
    square = tp_sum(jnp.sum(summed * summed, -1))
    out = (
        local_rows.astype(jnp.float32)
        + summed * lax.rsqrt(square[:, None] / full_width + norm_eps) * post_gain
    ).astype(jnp.bfloat16)
    return (
        out[:prompt_rows].reshape(seqs, pos_dev, width_local),
        out[prompt_rows:],
    )


def solution(mesh):
    in_specs = (
        P(None, "seq", "tp"),
        P(None, "tp"),
        P(None, None, "tp"),
        P("tp", None),
        P("tp"),
        P("tp"),
        P("tp"),
        P(),
    )
    out_specs = (P(None, "seq", "tp"), P(None, "tp"))
    return jax.shard_map(body, mesh=mesh, in_specs=in_specs, out_specs=out_specs, check_vma=False)
```

profile of v0, /device:TPU:32, one launch (start us, length us, event | category | flops | bytes accessed | tf_op | source)
XLA Modules:
  0.0 196.7 jit_solution(10754987210821596228)
XLA Ops:
  0.6 1.1 pad_maximum_fusion.4
  1.7 3.1 %collective-permute-start.2 = (bf16[516,512]{1,0:T(8,128)(2,1)S(1)}, bf16[516,512]{1,0:T(8,128)(2,1)}, u32[]{:S(2)}, u32[]{:S(2)}) collective-permute-start(bf16[516,512]{1,0:T(8,128)(2,1)S(1)} %pad_maximum_fusion.4), channel_id=1, source_target_pairs={{0,6},{1,7},{2,0},{3,1},{4,2},{5,3},{6,4},{7,5},{8,14},{9,15},{10,... | collective-permute-start | bytes 1585160 | tf_op jit(solution)/shard_map/ppermute | solution.py:53
  4.8 1.5 collective-permute-start
  6.4 0.7 add_convert_fusion.1
  7.1 6.5 %constant_dynamic-slice_fusion.12 = (bf16[3,512,512]{2,1,0:T(8,128)(2,1)S(1)}, bf16[3,512,512]{2,1,0:T(8,128)(2,1)S(1)}, bf16[3,512,512]{2,1,0:T(8,128)(2,1)S(1)...) fusion(bf16[3,4096,512]{2,1,0:T(8,128)(2,1)} %param.10, ...), kind=kLoop, calls=%fused_computation.142 | loop fusion | bytes 22020124 | tf_op jit(solution)/shard_map/dynamic_slice | solution.py:180
  13.7 4.8 %collective-permute-done = bf16[516,512]{1,0:T(8,128)(2,1)} collective-permute-done((bf16[516,512]{1,0:T(8,128)(2,1)S(1)}, bf16[516,512]{1,0:T(8,128)(2,1)}, u32[]{:S(2)}, u32[]{:S(2)}) %collective-permute-start) | collective-permute-done | bytes 528416 | tf_op jit(solution)/shard_map/ppermute | solution.py:53
  18.5 1.0 slice.258
  19.6 1.1 slice.255
  20.9 3.0 %collective-permute-start.4 = (bf16[516,512]{1,0:T(8,128)(2,1)S(1)}, bf16[516,512]{1,0:T(8,128)(2,1)S(1)}, u32[]{:S(2)}, u32[]{:S(2)}) collective-permute-start(bf16[516,512]{1,0:T(8,128)(2,1)S(1)} %get-tuple-element.46), channel_id=1, source_target_pairs={{0,6},{1,7},{2,0},{3,1},{4,2},{5,3},{6,4},{7,5},{8,14},{9,15},{10,... | collective-permute-start | bytes 1585160 | tf_op jit(solution)/shard_map/ppermute | solution.py:53
  23.9 1.5 collective-permute-start.3
  25.4 4.9 %fusion.2 = f32[3,512,516]{1,2,0:T(8,128)S(1)} fusion(bf16[3,512,512]{2,1,0:T(8,128)(2,1)S(1)} %get-tuple-element.10, bf16[3,512,512]{2,1,0:T(8,128)(2,1)S(1)} %get-tuple-element.11, bf16[3,512,512]{2,1,0:T(8,128)(2,1)S(1)} %copy-done.2, bf16[3,512,512]{2,1,0:T(8,128)(2,1)S(1)} %copy-done.3, bf16[516,512]{1,0:T(8,128)(2,1)} %collective-permute-done.2, ...), kind=kOutput, calls=%fused_computation.5 | convolution fusion | flops 3282124800 | bytes 11575296 | tf_op jit(solution)/shard_map/tn,cnf->ctf/dot_general | solution.py:188
  30.3 8.1 %collective-permute-done.5 = bf16[516,512]{1,0:T(8,128)(2,1)S(1)} collective-permute-done((bf16[516,512]{1,0:T(8,128)(2,1)S(1)}, bf16[516,512]{1,0:T(8,128)(2,1)S(1)}, u32[]{:S(2)}, u32[]{:S(2)}) %collective-permute-start.5) | collective-permute-done | bytes 528416 | tf_op jit(solution)/shard_map/ppermute | solution.py:53
  38.5 3.3 %collective-permute-start.7 = (bf16[516,128]{1,0:T(8,128)(2,1)S(1)}, bf16[516,128]{1,0:T(8,128)(2,1)S(1)}, u32[]{:S(2)}, u32[]{:S(2)}) collective-permute-start(bf16[516,128]{1,0:T(8,128)(2,1)S(1)} %slice.265), channel_id=1, source_target_pairs={{0,6},{1,7},{2,0},{3,1},{4,2},{5,3},{6,4},{7,5},{8,14},{9,15},{10,... | collective-permute-start | bytes 396296 | tf_op jit(solution)/shard_map/ppermute | solution.py:53
  41.9 0.8 collective-permute-start.6
  42.8 2.8 %fusion.10 = f32[3,512,516]{1,2,0:T(8,128)S(1)} fusion(bf16[3,512,512]{2,1,0:T(8,128)(2,1)S(1)} %get-tuple-element.14, bf16[3,512,512]{2,1,0:T(8,128)(2,1)S(1)} %get-tuple-element.9, bf16[3,512,512]{2,1,0:T(8,128)(2,1)S(1)} %get-tuple-element.8, bf16[516,1536]{1,0:T(8,128)(2,1)S(1)} %slice_dynamic-update-slice_fusion), kind=kOutput, calls=%fused_computation.13 | convolution fusion | flops 2448949248 | bytes 9474048 | tf_op jit(solution)/shard_map/tn,cnf->ctf/dot_general | solution.py:188
  45.6 3.0 %collective-permute-done.6 = bf16[516,256]{1,0:T(8,128)(2,1)S(1)} collective-permute-done((bf16[516,256]{1,0:T(8,128)(2,1)S(1)}, bf16[516,256]{1,0:T(8,128)(2,1)S(1)}, u32[]{:S(2)}, u32[]{:S(2)}) %collective-permute-start.6) | collective-permute-done | bytes 264224 | tf_op jit(solution)/shard_map/ppermute | solution.py:53
  48.6 2.7 %add_bitcast_fusion.proj_ref = f32[3,516,512]{2,1,0:T(8,128)S(1)} fusion(f32[3,512,516]{1,2,0:T(8,128)S(1)} %fusion.2, f32[3,512,516]{1,2,0:T(8,128)S(1)} %fusion.10, bf16[3,4096,512]{2,1,0:T(8,128)(2,1)} %param.10, s32[]{:T(128)S(6)} %select_n.114, bf16[516,128]{1,0:T(8,128)(2,1)S(1)} %collective-permute-done.8, ...), kind=kOutput, calls=%fused_computation.26 | convolution fusion | flops 814768128 | bytes 11612164 | tf_op jit(solution)/shard_map/tn,cnf->ctf/dot_general | solution.py:188
  51.6 0.6 collective-permute-start.12
  52.2 1.5 collective-permute-start.9
  53.7 1.0 fusion.82
  55.9 1.5 collective-permute-start.10
  57.3 1.0 pad_maximum_fusion.12
  59.5 3.0 %collective-permute-start.11 = (f32[516]{0:T(1024)S(1)}, f32[516]{0:T(1024)S(1)}, u32[]{:S(2)}, u32[]{:S(2)}) collective-permute-start(f32[516]{0:T(1024)S(1)} %add.236), channel_id=1, source_target_pairs={{0,4},{1,5},{2,6},{3,7},{4,0},{5,1},{6,2},{7,3},{8,12},{9,13},{10,... | collective-permute-start | bytes 6200 | tf_op jit(solution)/shard_map/ppermute | solution.py:93
  62.5 0.6 broadcast_in_dim.43.gain_ref
  63.1 1.0 collective-permute-done.14
  64.6 1.1 copy.10.square_ref
  65.7 4.1 %shard_map.95 = (bf16[16,3,128,128]{3,2,1,0:T(8,128)(2,1)}, f32[3,4,512]{2,1,0:T(4,128)}) custom-call(f32[3,516,512]{2,1,0:T(8,128)} %copy-done, f32[2,516,1]{2,1,0:T(8,128)} %copy.10.square_ref, f32[2,1,512]{2,1,0:T(1,128)} %broadcast_in_dim.43.gain_ref, f32[516,128]{1,0:T(8,128)} %get-tuple-element.61.cos_ref, f32[516,128]{1,0:T(8,128)} %get-tuple-element.62.sin_ref), custom_call_target="tpu_custom_call" | custom-call | tf_op jit(solution)/shard_map/pallas_call | solution.py:118
  69.8 8.0 %all-to-all-start = ((bf16[16,3,128,128]{3,2,1,0:T(8,128)(2,1)}), bf16[16,3,128,128]{3,2,1,0:T(8,128)(2,1)S(1)}, u32[]{:S(2)}, u32[]{:S(2)}) async-start(bf16[16,3,128,128]{3,2,1,0:T(8,128)(2,1)} %get-tuple-element.4), calls=%async_computation | async-start | bytes 3145728 | tf_op jit(solution)/shard_map/all_to_all | solution.py:217
  78.4 0.6 iota_compare_fusion.3
  79.0 0.7 iota_compare_fusion.2
  79.8 0.6 fusion.91
  81.0 16.8 %all-to-all-done = bf16[16,3,128,128]{3,2,1,0:T(8,128)(2,1)S(1)} async-done(((bf16[16,3,128,128]{3,2,1,0:T(8,128)(2,1)}), bf16[16,3,128,128]{3,2,1,0:T(8,128)(2,1)S(1)}, u32[]{:S(2)}, u32[]{:S(2)}) %all-to-all-start) | async-done | bytes 1572896 | tf_op jit(solution)/shard_map/all_to_all | solution.py:217
  98.2 1.3 fusion.83
  100.1 1.3 fusion.86
  101.4 0.9 fusion.108
  103.0 3.9 %fusion.1 = (f32[1024]{0:T(1024)S(1)}, f32[1024,2048]{1,0:T(8,128)S(1)}) fusion(s32[1024]{0:T(1024)S(1)} %iota_add_fusion, pred[2048]{0:T(1024)(128)(4,1)S(1)} %iota_compare_fusion.2, bf16[1024,128]{1,0:T(8,128)(2,1)} %bitcast.97, bf16[2048,128]{1,0:T(8,128)(2,1)S(1)} %bitcast.92), kind=kOutput, calls=%fused_computation.4 | convolution fusion | flops 547355648 | bytes 9185280 | tf_op jit(solution)/shard_map/dot_general | solution.py:136
  107.0 3.9 %fusion.105 = f32[1024]{0:T(1024)S(1)} fusion(f32[1024]{0:T(1024)S(1)} %get-tuple-element.53, f32[1024,2048]{1,0:T(8,128)S(1)} %get-tuple-element.54, pred[2048]{0:T(1024)(128)(4,1)S(1)} %iota_compare_fusion.2, s32[1024]{0:T(1024)S(1)} %iota_add_fusion), kind=kLoop, calls=%fused_computation.175 | loop fusion | flops 14679040 | bytes 8402944 | tf_op jit(solution)/shard_map/reduce_sum | solution.py:145
  110.9 3.6 %fusion.55 = bf16[1024,128]{1,0:T(8,128)(2,1)S(1)} fusion(bf16[2048,128]{1,0:T(8,128)(2,1)S(1)} %bitcast.89, f32[1024]{0:T(1024)S(1)} %fusion.105, f32[1024,2048]{1,0:T(8,128)S(1)} %get-tuple-element.54, f32[1024]{0:T(1024)S(1)} %get-tuple-element.53, s32[1024]{0:T(1024)S(1)} %iota_add_fusion, pred[2048]{0:T(1024)(128)(4,1)S(1)} %iota_compare_fusion.2), kind=kOutput, calls=%fused_computation.58 | convolution fusion | flops 551813120 | bytes 9189376 | tf_op jit(solution)/shard_map/dot_general | solution.py:147
  114.5 1.6 fusion.19
  116.1 2.1 %fusion.68 = f32[1024]{0:T(1024)S(1)} fusion(f32[1024]{0:T(1024)S(1)} %get-tuple-element.55, f32[1024,1024]{0,1:T(8,128)S(1)} %get-tuple-element.56, pred[1024]{0:T(1024)(128)(4,1)S(1)} %iota_compare_fusion.3), kind=kLoop, calls=%fused_computation.73 | loop fusion | flops 7339008 | bytes 4203520 | tf_op jit(solution)/shard_map/reduce_sum | solution.py:145
  118.2 1.1 fusion.58
  119.6 0.8 pad_maximum_fusion.2
  120.4 8.1 %all-to-all-start.1 = ((bf16[16,136,128]{2,1,0:T(8,128)(2,1)}), bf16[16,136,128]{2,1,0:T(8,128)(2,1)S(1)}, u32[]{:S(2)}, u32[]{:S(2)}) async-start(bf16[16,136,128]{2,1,0:T(8,128)(2,1)} %pad_maximum_fusion.2), calls=%async_computation.1 | async-start | bytes 1114112 | tf_op jit(solution)/shard_map/all_to_all | solution.py:232
  128.5 3.3 %constant_dynamic-slice_fusion.6 = (bf16[512,512]{1,0:T(8,128)(2,1)S(1)}, bf16[512,512]{1,0:T(8,128)(2,1)S(1)}, bf16[512,512]{1,0:T(8,128)(2,1)S(1)}, bf16[512,5...) fusion(bf16[512,4096]{1,0:T(8,128)(2,1)} %param.11, ...), kind=kLoop, calls=%fused_computation.135 | loop fusion | bytes 7340060 | tf_op jit(solution)/shard_map/dynamic_slice | solution.py:180
  131.8 5.8 %all-to-all-done.1 = bf16[16,136,128]{2,1,0:T(8,128)(2,1)S(1)} async-done(((bf16[16,136,128]{2,1,0:T(8,128)(2,1)}), bf16[16,136,128]{2,1,0:T(8,128)(2,1)S(1)}, u32[]{:S(2)}, u32[]{:S(2)}) %all-to-all-start.1) | async-done | bytes 557088 | tf_op jit(solution)/shard_map/all_to_all | solution.py:232
  138.1 1.5 convolution_convert_fusion
  139.6 1.3 collective-permute-start.15
  140.9 2.0 %collective-permute-start.18 = (bf16[516,128]{1,0:T(8,128)(2,1)S(1)}, bf16[516,128]{1,0:T(8,128)(2,1)S(1)}, u32[]{:S(2)}, u32[]{:S(2)}) collective-permute-start(bf16[516,128]{1,0:T(8,128)(2,1)S(1)} %get-tuple-element.40), channel_id=1, source_target_pairs={{0,6},{1,7},{2,0},{3,1},{4,2},{5,3},{6,4},{7,5},{8,14},{9,15},{10,... | collective-permute-start | bytes 396296 | tf_op jit(solution)/shard_map/ppermute | solution.py:73
  142.9 1.0 fusion.113
  144.1 0.7 collective-permute-start.16
  144.8 1.8 collective-permute-start.21
  147.3 3.0 %collective-permute-start.19 = (bf16[516,512]{1,0:T(8,128)(2,1)S(1)}, bf16[516,512]{1,0:T(8,128)(2,1)S(1)}, u32[]{:S(2)}, u32[]{:S(2)}) collective-permute-start(bf16[516,512]{1,0:T(8,128)(2,1)S(1)} %fusion.73), channel_id=1, source_target_pairs={{0,6},{1,7},{2,0},{3,1},{4,2},{5,3},{6,4},{7,5},{8,14},{9,15},{10,... | collective-permute-start | bytes 1585160 | tf_op jit(solution)/shard_map/ppermute | solution.py:73
  150.3 3.4 %collective-permute-done.16 = bf16[516,256]{1,0:T(8,128)(2,1)S(1)} collective-permute-done((bf16[516,256]{1,0:T(8,128)(2,1)S(1)}, bf16[516,256]{1,0:T(8,128)(2,1)S(1)}, u32[]{:S(2)}, u32[]{:S(2)}) %collective-permute-start.16) | collective-permute-done | bytes 264224 | tf_op jit(solution)/shard_map/ppermute | solution.py:73
  153.9 1.3 fusion.114
  155.3 9.1 %collective-permute-done.21 = bf16[516,512]{1,0:T(8,128)(2,1)S(1)} collective-permute-done((bf16[516,512]{1,0:T(8,128)(2,1)S(1)}, bf16[516,512]{1,0:T(8,128)(2,1)S(1)}, u32[]{:S(2)}, u32[]{:S(2)}) %collective-permute-start.21) | collective-permute-done | bytes 528416 | tf_op jit(solution)/shard_map/ppermute | solution.py:73
  164.6 3.1 %collective-permute-done.17 = bf16[516,512]{1,0:T(8,128)(2,1)S(1)} collective-permute-done((bf16[516,512]{1,0:T(8,128)(2,1)S(1)}, bf16[516,512]{1,0:T(8,128)(2,1)S(1)}, u32[]{:S(2)}, u32[]{:S(2)}) %collective-permute-start.17) | collective-permute-done | bytes 528416 | tf_op jit(solution)/shard_map/ppermute | solution.py:73
  168.6 2.1 %collective-permute-start.22 = (bf16[516,512]{1,0:T(8,128)(2,1)S(1)}, bf16[516,512]{1,0:T(8,128)(2,1)S(1)}, u32[]{:S(2)}, u32[]{:S(2)}) collective-permute-start(bf16[516,512]{1,0:T(8,128)(2,1)S(1)} %pad_maximum_fusion.9), channel_id=1, source_target_pairs={{0,2},{1,3},{2,4},{3,5},{4,6},{5,7},{6,0},{7,1},{8,10},{9,11},{10,... | collective-permute-start | bytes 1585160 | tf_op jit(solution)/shard_map/ppermute | solution.py:73
  171.2 9.1 %collective-permute-done.23 = bf16[516,512]{1,0:T(8,128)(2,1)S(1)} collective-permute-done((bf16[516,512]{1,0:T(8,128)(2,1)S(1)}, bf16[516,512]{1,0:T(8,128)(2,1)S(1)}, u32[]{:S(2)}, u32[]{:S(2)}) %collective-permute-start.23) | collective-permute-done | bytes 528416 | tf_op jit(solution)/shard_map/ppermute | solution.py:73
  180.3 1.3 collective-permute-done.22
  182.9 3.3 %collective-permute-done.24 = f32[516]{0:T(1024)S(1)} collective-permute-done((f32[516]{0:T(1024)S(1)}, f32[516]{0:T(1024)S(1)}, u32[]{:S(2)}, u32[]{:S(2)}) %collective-permute-start.24) | collective-permute-done | bytes 2096 | tf_op jit(solution)/shard_map/ppermute | solution.py:93
  186.4 3.3 %collective-permute-done.25 = f32[516]{0:T(1024)S(1)} collective-permute-done((f32[516]{0:T(1024)S(1)}, f32[516]{0:T(1024)S(1)}, u32[]{:S(2)}, u32[]{:S(2)}) %collective-permute-start.25) | collective-permute-done | bytes 2096 | tf_op jit(solution)/shard_map/ppermute | solution.py:93
  189.7 0.9 collective-permute-start.26
  190.7 4.2 %collective-permute-done.26 = f32[516]{0:T(1024)S(1)} collective-permute-done((f32[516]{0:T(1024)S(1)}, f32[516]{0:T(1024)S(1)}, u32[]{:S(2)}, u32[]{:S(2)}) %collective-permute-start.26) | collective-permute-done | bytes 2096 | tf_op jit(solution)/shard_map/ppermute | solution.py:93
  195.3 0.8 slice.301
  (119 shorter events, 10.5 us)
Async XLA Ops:
  1.7 17.9 %collective-permute-start.2 = (bf16[516,512]{1,0:T(8,128)(2,1)S(1)}, bf16[516,512]{1,0:T(8,128)(2,1)}, u32[]{:S(2)}, u32[]{:S(2)}) collective-permute-start(bf16[516,512]{1,0:T(8,128)(2,1)S(1)} %pad_maximum_fusion.4), channel_id=1, source_target_pairs={{0,6},{1,7},{2,0},{3,1},{4,2},{5,3},{6,4},{7,5},{8,14},{9,15},{10,... | collective-permute-start | bytes 1585160 | tf_op jit(solution)/shard_map/ppermute | solution.py:53
  4.8 14.8 %collective-permute-start.1 = (bf16[516,512]{1,0:T(8,128)(2,1)S(1)}, bf16[516,512]{1,0:T(8,128)(2,1)S(1)}, u32[]{:S(2)}, u32[]{:S(2)}) collective-permute-start(bf16[516,512]{1,0:T(8,128)(2,1)S(1)} %pad_maximum_fusion.4), channel_id=1, source_target_pairs={{0,2},{1,3},{2,4},{3,5},{4,6},{5,7},{6,0},{7,1},{8,10},{9,11},{10,... | collective-permute-start | bytes 1585160 | tf_op jit(solution)/shard_map/ppermute | solution.py:53
  4.8 13.7 %collective-permute-start = (bf16[516,512]{1,0:T(8,128)(2,1)S(1)}, bf16[516,512]{1,0:T(8,128)(2,1)}, u32[]{:S(2)}, u32[]{:S(2)}) collective-permute-start(bf16[516,512]{1,0:T(8,128)(2,1)S(1)} %pad_maximum_fusion.4), channel_id=1, source_target_pairs={{0,1},{1,0},{2,3},{3,2},{4,5},{5,4},{6,7},{7,6},{8,9},{9,8},{10,11... | collective-permute-start | bytes 1585160 | tf_op jit(solution)/shard_map/ppermute | solution.py:53
  19.5 5.9 %copy-start.1 = (bf16[4,128,512]{2,1,0:T(8,128)(2,1)S(1)}, bf16[4,128,512]{2,1,0:T(8,128)(2,1)}, u32[]{:S(2)}) copy-start(bf16[4,128,512]{2,1,0:T(8,128)(2,1)} %param.8) | copy-start | bytes 1572868
  19.5 5.9 %copy-start.2 = (bf16[3,512,512]{2,1,0:T(8,128)(2,1)S(1)}, bf16[3,512,512]{2,1,0:T(8,128)(2,1)}, u32[]{:S(2)}) copy-start(bf16[3,512,512]{2,1,0:T(8,128)(2,1)} %get-tuple-element.12) | copy-start | bytes 4718596
  19.5 5.9 %copy-start.3 = (bf16[3,512,512]{2,1,0:T(8,128)(2,1)S(1)}, bf16[3,512,512]{2,1,0:T(8,128)(2,1)}, u32[]{:S(2)}) copy-start(bf16[3,512,512]{2,1,0:T(8,128)(2,1)} %get-tuple-element.13) | copy-start | bytes 4718596
  19.5 5.9 %copy-start.10 = (bf16[4,512]{1,0:T(4,128)(2,1)S(1)}, bf16[4,512]{1,0:T(4,128)(2,1)}, u32[]{:S(2)}) copy-start(bf16[4,512]{1,0:T(4,128)(2,1)} %param.9) | copy-start | bytes 12292
  20.9 17.6 %collective-permute-start.4 = (bf16[516,512]{1,0:T(8,128)(2,1)S(1)}, bf16[516,512]{1,0:T(8,128)(2,1)S(1)}, u32[]{:S(2)}, u32[]{:S(2)}) collective-permute-start(bf16[516,512]{1,0:T(8,128)(2,1)S(1)} %get-tuple-element.46), channel_id=1, source_target_pairs={{0,6},{1,7},{2,0},{3,1},{4,2},{5,3},{6,4},{7,5},{8,14},{9,15},{10,... | collective-permute-start | bytes 1585160 | tf_op jit(solution)/shard_map/ppermute | solution.py:53
  23.9 17.9 %collective-permute-start.3 = (bf16[516,512]{1,0:T(8,128)(2,1)S(1)}, bf16[516,512]{1,0:T(8,128)(2,1)S(1)}, u32[]{:S(2)}, u32[]{:S(2)}) collective-permute-start(bf16[516,512]{1,0:T(8,128)(2,1)S(1)} %get-tuple-element.47), channel_id=1, source_target_pairs={{0,1},{1,0},{2,3},{3,2},{4,5},{5,4},{6,7},{7,6},{8,9},{9,8},{10,11... | collective-permute-start | bytes 1585160 | tf_op jit(solution)/shard_map/ppermute | solution.py:53
  25.4 13.0 %collective-permute-start.5 = (bf16[516,512]{1,0:T(8,128)(2,1)S(1)}, bf16[516,512]{1,0:T(8,128)(2,1)S(1)}, u32[]{:S(2)}, u32[]{:S(2)}) collective-permute-start(bf16[516,512]{1,0:T(8,128)(2,1)S(1)} %get-tuple-element.45), channel_id=1, source_target_pairs={{0,2},{1,3},{2,4},{3,5},{4,6},{5,7},{6,0},{7,1},{8,10},{9,11},{10,... | collective-permute-start | bytes 1585160 | tf_op jit(solution)/shard_map/ppermute | solution.py:53
  38.4 7.2 %collective-permute-start.8 = (bf16[516,128]{1,0:T(8,128)(2,1)S(1)}, bf16[516,128]{1,0:T(8,128)(2,1)S(1)}, u32[]{:S(2)}, u32[]{:S(2)}) collective-permute-start(bf16[516,128]{1,0:T(8,128)(2,1)S(1)} %slice.266), channel_id=1, source_target_pairs={{0,2},{1,3},{2,4},{3,5},{4,6},{5,7},{6,0},{7,1},{8,10},{9,11},{10,... | collective-permute-start | bytes 396296 | tf_op jit(solution)/shard_map/ppermute | solution.py:53
  38.5 7.1 %collective-permute-start.7 = (bf16[516,128]{1,0:T(8,128)(2,1)S(1)}, bf16[516,128]{1,0:T(8,128)(2,1)S(1)}, u32[]{:S(2)}, u32[]{:S(2)}) collective-permute-start(bf16[516,128]{1,0:T(8,128)(2,1)S(1)} %slice.265), channel_id=1, source_target_pairs={{0,6},{1,7},{2,0},{3,1},{4,2},{5,3},{6,4},{7,5},{8,14},{9,15},{10,... | collective-permute-start | bytes 396296 | tf_op jit(solution)/shard_map/ppermute | solution.py:53
  41.9 6.7 %collective-permute-start.6 = (bf16[516,256]{1,0:T(8,128)(2,1)S(1)}, bf16[516,256]{1,0:T(8,128)(2,1)S(1)}, u32[]{:S(2)}, u32[]{:S(2)}) collective-permute-start(bf16[516,256]{1,0:T(8,128)(2,1)S(1)} %get-tuple-element.41), channel_id=1, source_target_pairs={{0,1},{1,0},{2,3},{3,2},{4,5},{5,4},{6,7},{7,6},{8,9},{9,8},{10,11... | collective-permute-start | bytes 792584 | tf_op jit(solution)/shard_map/ppermute | solution.py:53
  51.3 7.0 %copy-start = (f32[3,516,512]{2,1,0:T(8,128)}, f32[3,516,512]{2,1,0:T(8,128)S(1)}, u32[]{:S(2)}) copy-start(f32[3,516,512]{2,1,0:T(8,128)S(1)} %add_bitcast_fusion.proj_ref) | copy-start | bytes 9510916
  51.3 11.1 %copy-start.12 = (f32[512]{0:T(512)S(1)}, f32[512]{0:T(512)}, u32[]{:S(2)}) copy-start(f32[512]{0:T(512)} %param.13) | copy-start | bytes 6148
  51.4 11.1 %copy-start.13 = (f32[512]{0:T(512)S(1)}, f32[512]{0:T(512)}, u32[]{:S(2)}) copy-start(f32[512]{0:T(512)} %param.12) | copy-start | bytes 6148
  51.6 3.7 %collective-permute-start.12 = (f32[516]{0:T(1024)S(1)}, f32[516]{0:T(1024)S(1)}, u32[]{:S(2)}, u32[]{:S(2)}) collective-permute-start(f32[516]{0:T(1024)S(1)} %get-tuple-element.7), channel_id=1, source_target_pairs={{0,1},{1,0},{2,3},{3,2},{4,5},{5,4},{6,7},{7,6},{8,9},{9,8},{10,11... | collective-permute-start | bytes 6200 | tf_op jit(solution)/shard_map/ppermute | solution.py:93
  52.2 3.6 %collective-permute-start.9 = (f32[516]{0:T(1024)S(1)}, f32[516]{0:T(1024)S(1)}, u32[]{:S(2)}, u32[]{:S(2)}) collective-permute-start(f32[516]{0:T(1024)S(1)} %get-tuple-element.6), channel_id=1, source_target_pairs={{0,1},{1,0},{2,3},{3,2},{4,5},{5,4},{6,7},{7,6},{8,9},{9,8},{10,11... | collective-permute-start | bytes 6200 | tf_op jit(solution)/shard_map/ppermute | solution.py:93
  55.3 3.6 %collective-permute-start.13 = (f32[516]{0:T(1024)S(1)}, f32[516]{0:T(1024)S(1)}, u32[]{:S(2)}, u32[]{:S(2)}) collective-permute-start(f32[516]{0:T(1024)S(1)} %add.238), channel_id=1, source_target_pairs={{0,2},{1,3},{2,0},{3,1},{4,6},{5,7},{6,4},{7,5},{8,10},{9,11},{10,... | collective-permute-start | bytes 6200 | tf_op jit(solution)/shard_map/ppermute | solution.py:93
  55.9 3.6 %collective-permute-start.10 = (f32[516]{0:T(1024)S(1)}, f32[516]{0:T(1024)S(1)}, u32[]{:S(2)}, u32[]{:S(2)}) collective-permute-start(f32[516]{0:T(1024)S(1)} %add.235), channel_id=1, source_target_pairs={{0,2},{1,3},{2,0},{3,1},{4,6},{5,7},{6,4},{7,5},{8,10},{9,11},{10,... | collective-permute-start | bytes 6200 | tf_op jit(solution)/shard_map/ppermute | solution.py:93
  58.9 5.1 %collective-permute-start.14 = (f32[516]{0:T(1024)S(1)}, f32[516]{0:T(1024)S(1)}, u32[]{:S(2)}, u32[]{:S(2)}) collective-permute-start(f32[516]{0:T(1024)S(1)} %add.239), channel_id=1, source_target_pairs={{0,4},{1,5},{2,6},{3,7},{4,0},{5,1},{6,2},{7,3},{8,12},{9,13},{10,... | collective-permute-start | bytes 6200 | tf_op jit(solution)/shard_map/ppermute | solution.py:93
  59.5 5.1 %collective-permute-start.11 = (f32[516]{0:T(1024)S(1)}, f32[516]{0:T(1024)S(1)}, u32[]{:S(2)}, u32[]{:S(2)}) collective-permute-start(f32[516]{0:T(1024)S(1)} %add.236), channel_id=1, source_target_pairs={{0,4},{1,5},{2,6},{3,7},{4,0},{5,1},{6,2},{7,3},{8,12},{9,13},{10,... | collective-permute-start | bytes 6200 | tf_op jit(solution)/shard_map/ppermute | solution.py:93
  69.8 8.0 %copy-start.14 = (s32[4]{0:T(128)S(1)}, s32[4]{0:T(128)}, u32[]{:S(2)}) copy-start(s32[4]{0:T(128)} %param.15) | copy-start | bytes 52
  69.8 9.9 %copy-start.9 = (f32[3,4,512]{2,1,0:T(4,128)S(1)}, f32[3,4,512]{2,1,0:T(4,128)}, u32[]{:S(2)}) copy-start(f32[3,4,512]{2,1,0:T(4,128)} %get-tuple-element.5) | copy-start | bytes 73732
  69.8 28.1 %all-to-all-start = ((bf16[16,3,128,128]{3,2,1,0:T(8,128)(2,1)}), bf16[16,3,128,128]{3,2,1,0:T(8,128)(2,1)S(1)}, u32[]{:S(2)}, u32[]{:S(2)}) async-start(bf16[16,3,128,128]{3,2,1,0:T(8,128)(2,1)} %get-tuple-element.4), calls=%async_computation | async-start | bytes 3145728 | tf_op jit(solution)/shard_map/all_to_all | solution.py:217
  110.9 3.6 %copy-start.7 = (bf16[1,8,128,128]{3,2,0,1:T(8,128)(2,1)S(1)}, bf16[1,8,128,128]{3,2,0,1:T(8,128)(2,1)}, u32[]{:S(2)}) copy-start(bf16[1,8,128,128]{3,2,0,1:T(8,128)(2,1)} %get-tuple-element.33) | copy-start | bytes 786436
  110.9 3.6 %copy-start.8 = (bf16[1,8,128,128]{3,2,0,1:T(8,128)(2,1)S(1)}, bf16[1,8,128,128]{3,2,0,1:T(8,128)(2,1)}, u32[]{:S(2)}) copy-start(bf16[1,8,128,128]{3,2,0,1:T(8,128)(2,1)} %get-tuple-element.36) | copy-start | bytes 786436
  120.4 17.1 %all-to-all-start.1 = ((bf16[16,136,128]{2,1,0:T(8,128)(2,1)}), bf16[16,136,128]{2,1,0:T(8,128)(2,1)S(1)}, u32[]{:S(2)}, u32[]{:S(2)}) async-start(bf16[16,136,128]{2,1,0:T(8,128)(2,1)} %pad_maximum_fusion.2), calls=%async_computation.1 | async-start | bytes 1114112 | tf_op jit(solution)/shard_map/all_to_all | solution.py:232
  139.6 7.5 %collective-permute-start.15 = (bf16[516,128]{1,0:T(8,128)(2,1)S(1)}, bf16[516,128]{1,0:T(8,128)(2,1)S(1)}, u32[]{:S(2)}, u32[]{:S(2)}) collective-permute-start(bf16[516,128]{1,0:T(8,128)(2,1)S(1)} %get-tuple-element.39), channel_id=1, source_target_pairs={{0,2},{1,3},{2,4},{3,5},{4,6},{5,7},{6,0},{7,1},{8,10},{9,11},{10,... | collective-permute-start | bytes 396296 | tf_op jit(solution)/shard_map/ppermute | solution.py:73
  140.9 6.2 %collective-permute-start.18 = (bf16[516,128]{1,0:T(8,128)(2,1)S(1)}, bf16[516,128]{1,0:T(8,128)(2,1)S(1)}, u32[]{:S(2)}, u32[]{:S(2)}) collective-permute-start(bf16[516,128]{1,0:T(8,128)(2,1)S(1)} %get-tuple-element.40), channel_id=1, source_target_pairs={{0,6},{1,7},{2,0},{3,1},{4,2},{5,3},{6,4},{7,5},{8,14},{9,15},{10,... | collective-permute-start | bytes 396296 | tf_op jit(solution)/shard_map/ppermute | solution.py:73
  144.1 9.6 %collective-permute-start.16 = (bf16[516,256]{1,0:T(8,128)(2,1)S(1)}, bf16[516,256]{1,0:T(8,128)(2,1)S(1)}, u32[]{:S(2)}, u32[]{:S(2)}) collective-permute-start(bf16[516,256]{1,0:T(8,128)(2,1)S(1)} %slice.284), channel_id=1, source_target_pairs={{0,1},{1,0},{2,3},{3,2},{4,5},{5,4},{6,7},{7,6},{8,9},{9,8},{10,11... | collective-permute-start | bytes 792584 | tf_op jit(solution)/shard_map/ppermute | solution.py:73
  144.8 19.5 %collective-permute-start.21 = (bf16[516,512]{1,0:T(8,128)(2,1)S(1)}, bf16[516,512]{1,0:T(8,128)(2,1)S(1)}, u32[]{:S(2)}, u32[]{:S(2)}) collective-permute-start(bf16[516,512]{1,0:T(8,128)(2,1)S(1)} %pad_maximum_fusion.8), channel_id=1, source_target_pairs={{0,1},{1,0},{2,3},{3,2},{4,5},{5,4},{6,7},{7,6},{8,9},{9,8},{10,11... | collective-permute-start | bytes 1585160 | tf_op jit(solution)/shard_map/ppermute | solution.py:73
  147.1 6.8 %copy-start.4 = (bf16[512,512]{1,0:T(8,128)(2,1)S(1)}, bf16[512,512]{1,0:T(8,128)(2,1)}, u32[]{:S(2)}) copy-start(bf16[512,512]{1,0:T(8,128)(2,1)} %get-tuple-element.22) | copy-start | bytes 1572868
  147.1 6.8 %copy-start.5 = (bf16[512,512]{1,0:T(8,128)(2,1)S(1)}, bf16[512,512]{1,0:T(8,128)(2,1)}, u32[]{:S(2)}) copy-start(bf16[512,512]{1,0:T(8,128)(2,1)} %get-tuple-element.23) | copy-start | bytes 1572868
  147.1 6.8 %copy-start.6 = (bf16[512,512]{1,0:T(8,128)(2,1)S(1)}, bf16[512,512]{1,0:T(8,128)(2,1)}, u32[]{:S(2)}) copy-start(bf16[512,512]{1,0:T(8,128)(2,1)} %get-tuple-element.24) | copy-start | bytes 1572868
  147.3 17.2 %collective-permute-start.19 = (bf16[516,512]{1,0:T(8,128)(2,1)S(1)}, bf16[516,512]{1,0:T(8,128)(2,1)S(1)}, u32[]{:S(2)}, u32[]{:S(2)}) collective-permute-start(bf16[516,512]{1,0:T(8,128)(2,1)S(1)} %fusion.73), channel_id=1, source_target_pairs={{0,6},{1,7},{2,0},{3,1},{4,2},{5,3},{6,4},{7,5},{8,14},{9,15},{10,... | collective-permute-start | bytes 1585160 | tf_op jit(solution)/shard_map/ppermute | solution.py:73
  153.8 14.0 %collective-permute-start.17 = (bf16[516,512]{1,0:T(8,128)(2,1)S(1)}, bf16[516,512]{1,0:T(8,128)(2,1)S(1)}, u32[]{:S(2)}, u32[]{:S(2)}) collective-permute-start(bf16[516,512]{1,0:T(8,128)(2,1)S(1)} %pad_maximum_fusion.6), channel_id=1, source_target_pairs={{0,2},{1,3},{2,4},{3,5},{4,6},{5,7},{6,0},{7,1},{8,10},{9,11},{10,... | collective-permute-start | bytes 1585160 | tf_op jit(solution)/shard_map/ppermute | solution.py:73
  168.5 11.8 %collective-permute-start.23 = (bf16[516,512]{1,0:T(8,128)(2,1)S(1)}, bf16[516,512]{1,0:T(8,128)(2,1)S(1)}, u32[]{:S(2)}, u32[]{:S(2)}) collective-permute-start(bf16[516,512]{1,0:T(8,128)(2,1)S(1)} %pad_maximum_fusion.10), channel_id=1, source_target_pairs={{0,6},{1,7},{2,0},{3,1},{4,2},{5,3},{6,4},{7,5},{8,14},{9,15},{10,... | collective-permute-start | bytes 1585160 | tf_op jit(solution)/shard_map/ppermute | solution.py:73
  168.6 26.2 %copy-start.11 = (f32[512]{0:T(512)S(1)}, f32[512]{0:T(512)}, u32[]{:S(2)}) copy-start(f32[512]{0:T(512)} %param.14) | copy-start | bytes 6148
  168.6 13.0 %collective-permute-start.22 = (bf16[516,512]{1,0:T(8,128)(2,1)S(1)}, bf16[516,512]{1,0:T(8,128)(2,1)S(1)}, u32[]{:S(2)}, u32[]{:S(2)}) collective-permute-start(bf16[516,512]{1,0:T(8,128)(2,1)S(1)} %pad_maximum_fusion.9), channel_id=1, source_target_pairs={{0,2},{1,3},{2,4},{3,5},{4,6},{5,7},{6,0},{7,1},{8,10},{9,11},{10,... | collective-permute-start | bytes 1585160 | tf_op jit(solution)/shard_map/ppermute | solution.py:73
  170.8 11.3 %collective-permute-start.20 = (bf16[516,512]{1,0:T(8,128)(2,1)S(1)}, bf16[516,512]{1,0:T(8,128)(2,1)S(1)}, u32[]{:S(2)}, u32[]{:S(2)}) collective-permute-start(bf16[516,512]{1,0:T(8,128)(2,1)S(1)} %pad_maximum_fusion.7), channel_id=1, source_target_pairs={{0,1},{1,0},{2,3},{3,2},{4,5},{5,4},{6,7},{7,6},{8,9},{9,8},{10,11... | collective-permute-start | bytes 1585160 | tf_op jit(solution)/shard_map/ppermute | solution.py:73
  182.4 3.7 %collective-permute-start.24 = (f32[516]{0:T(1024)S(1)}, f32[516]{0:T(1024)S(1)}, u32[]{:S(2)}, u32[]{:S(2)}) collective-permute-start(f32[516]{0:T(1024)S(1)} %multiply_reduce_fusion), channel_id=1, source_target_pairs={{0,1},{1,0},{2,3},{3,2},{4,5},{5,4},{6,7},{7,6},{8,9},{9,8},{10,11... | collective-permute-start | bytes 6200 | tf_op jit(solution)/shard_map/ppermute | solution.py:93
  186.1 3.6 %collective-permute-start.25 = (f32[516]{0:T(1024)S(1)}, f32[516]{0:T(1024)S(1)}, u32[]{:S(2)}, u32[]{:S(2)}) collective-permute-start(f32[516]{0:T(1024)S(1)} %add.260), channel_id=1, source_target_pairs={{0,2},{1,3},{2,0},{3,1},{4,6},{5,7},{6,4},{7,5},{8,10},{9,11},{10,... | collective-permute-start | bytes 6200 | tf_op jit(solution)/shard_map/ppermute | solution.py:93
  189.7 5.1 %collective-permute-start.26 = (f32[516]{0:T(1024)S(1)}, f32[516]{0:T(1024)S(1)}, u32[]{:S(2)}, u32[]{:S(2)}) collective-permute-start(f32[516]{0:T(1024)S(1)} %add.261), channel_id=1, source_target_pairs={{0,4},{1,5},{2,6},{3,7},{4,0},{5,1},{6,2},{7,3},{8,12},{9,13},{10,... | collective-permute-start | bytes 6200 | tf_op jit(solution)/shard_map/ppermute | solution.py:93
where the time goes:
time: 197 us
  waiting for transfers between devices  80 us (41%)
  starting transfers between devices  49 us (25%)
  matrix products  24.8 us (13%)
  other arithmetic  17.8 us (9%)
  local copies, waits for them, and re-layouts  17.7 us (9%)
  Pallas kernels  4.09 us (2%)
  between operations  3.38 us (2%)
    ppermute x9, waiting for transfers between devices, tp_reduce_scatter(): lax.ppermute(value.astype(jnp.bfloat16), 'tp', perm).astype(jnp.float32)  27 us
    all_to_all x1, waiting for transfers between devices, body(): got = lax.all_to_all(qkv, 'seq', 0, 0, tiled=True)  16.8 us
    ppermute x9, waiting for transfers between devices, tp_gather(): send = lambda value, perm: lax.ppermute(value, 'tp', perm)  16 us
    ppermute x9, waiting for transfers between devices, tp_sum(): lax.ppermute(v, 'tp', [(i, i ^ bit) for i in range(8)])  14.4 us
    ppermute x9, starting transfers between devices, tp_gather(): send = lambda value, perm: lax.ppermute(value, 'tp', perm)  13.2 us
    ppermute x9, starting transfers between devices, tp_reduce_scatter(): lax.ppermute(value.astype(jnp.bfloat16), 'tp', perm).astype(jnp.float32)  11.4 us
    dot_general x3, matrix products, body(): jnp.einsum('tn,cnf->ctf', jnp.concatenate(blocks, 1), jnp.concatenate(w_b...  10.4 us
    dynamic_slice x2, local copies, waits for them, and re-layouts, in_relative_order(): lax.dynamic_slice_in_dim(weight, order[name] * width_local, width_local,...  9.85 us
  transfers between devices with their start and end apart: 29, of which 22 were waited for; matrix products, arithmetic and copies ran while one was open for 14% of the time, Pallas kernels for 0%

commit v1 on v0

--- a/solution.py
+++ b/solution.py
@@ -11,17 +11,6 @@
 rope_base = 500000.0
 norm_eps = 1e-06
 masked_fill = -1e30
-
-
-def rotate(values, position):
-    half = values.shape[-1] // 2
-    freq = rope_base ** (-(jnp.arange(half, dtype=jnp.float32) * 2.0) / values.shape[-1])
-    angle = position.astype(jnp.float32)[..., None] * freq
-    cosine = jnp.cos(angle)
-    sine = jnp.sin(angle)
-    lower = values[..., :half]
-    upper = values[..., half:]
-    return jnp.concatenate([lower * cosine - upper * sine, upper * cosine + lower * sine], -1)
 
 
 RELATIVE = ("own", "ax", "aup", "adn", "m1", "m2", "m3", "m4")
@@ -194,7 +183,7 @@
         proj = term if proj is None else proj + term
         start = stop
     query_raw, key_raw = proj[0], proj[1]
-    query_sq, key_sq = tp_sum((jnp.sum(query_raw * query_raw, -1), jnp.sum(key_raw * key_raw, -1)))
+    squares = tp_sum(jnp.stack([jnp.sum(query_raw * query_raw, -1), jnp.sum(key_raw * key_raw, -1)]))
 
     seq_index = lax.axis_index("seq")
     query_pos = seq_index * pos_dev + jnp.arange(pos_dev, dtype=jnp.int32)
@@ -205,7 +194,7 @@
     cosine, sine = jnp.cos(angle), jnp.sin(angle)
     qkv, fresh = rope_pack(
         proj,
-        jnp.stack([query_sq, key_sq])[:, :, None],
+        squares[:, :, None],
         jnp.stack([q_gain, k_gain])[:, None, :],
         jnp.concatenate([cosine, cosine], 1),
         jnp.concatenate([-sine, sine], 1),

time: 197 us -> 197 us (level)
  starting transfers between devices: 49 us -> 43.9 us
  waiting for transfers between devices: 80 us -> 84.4 us
    ppermute x9 -> x6, starting transfers between devices: 8.28 us -> 3.3 us  [tp_sum(): lax.ppermute(v, 'tp', [(i, i ^ bit) for i in range(8)])]
    ppermute x9 -> x6, waiting for transfers between devices: 14.4 us -> 19 us  [tp_sum(): lax.ppermute(v, 'tp', [(i, i ^ bit) for i in range(8)])]
  transfers between devices with their start and end apart: 29 -> 26, of which waited for: 22 -> 19; matrix products, arithmetic and copies ran while one was open for 14% -> 14% of each run, Pallas kernels for 0% -> 0%
where the time goes in v1:
time: 197 us; the launch traced here: 196 us
  waiting for transfers between devices  84.4 us (43%)
  starting transfers between devices  43.9 us (22%)
  matrix products  24.8 us (13%)
  other arithmetic  17.8 us (9%)
  local copies, waits for them, and re-layouts  17.7 us (9%)
  Pallas kernels  4.1 us (2%)
  between operations  3.46 us (2%)
    ppermute x9, waiting for transfers between devices, tp_reduce_scatter(): lax.ppermute(value.astype(jnp.bfloat16), 'tp', perm).astype(jnp.float32)  26.8 us
    ppermute x6, waiting for transfers between devices, tp_sum(): lax.ppermute(v, 'tp', [(i, i ^ bit) for i in range(8)])  19 us
    all_to_all x1, waiting for transfers between devices, body(): got = lax.all_to_all(qkv, 'seq', 0, 0, tiled=True)  16.8 us
    ppermute x9, waiting for transfers between devices, tp_gather(): send = lambda value, perm: lax.ppermute(value, 'tp', perm)  16 us
    ppermute x9, starting transfers between devices, tp_gather(): send = lambda value, perm: lax.ppermute(value, 'tp', perm)  13.2 us
    ppermute x9, starting transfers between devices, tp_reduce_scatter(): lax.ppermute(value.astype(jnp.bfloat16), 'tp', perm).astype(jnp.float32)  11.7 us
    dot_general x3, matrix products, body(): jnp.einsum('tn,cnf->ctf', jnp.concatenate(blocks, 1), jnp.concatenate(w_b...  10.4 us
    dynamic_slice x2, local copies, waits for them, and re-layouts, in_relative_order(): lax.dynamic_slice_in_dim(weight, order[name] * width_local, width_local,...  9.9 us
  transfers between devices with their start and end apart: 26, of which 19 were waited for; matrix products, arithmetic and copies ran while one was open for 14% of the time, Pallas kernels for 0%

profile of v1, /device:TPU:32, one launch (start us, length us, event | category | flops | bytes accessed | tf_op | source)
XLA Modules:
  0.0 196.1 jit_solution(15886201472633929743)
XLA Ops:
  0.6 1.1 pad_maximum_fusion.4
  1.7 3.1 %collective-permute-start.2 = (bf16[516,512]{1,0:T(8,128)(2,1)S(1)}, bf16[516,512]{1,0:T(8,128)(2,1)}, u32[]{:S(2)}, u32[]{:S(2)}) collective-permute-start(bf16[516,512]{1,0:T(8,128)(2,1)S(1)} %pad_maximum_fusion.4), channel_id=1, source_target_pairs={{0,6},{1,7},{2,0},{3,1},{4,2},{5,3},{6,4},{7,5},{8,14},{9,15},{10,... | collective-permute-start | bytes 1585160 | tf_op jit(solution)/shard_map/ppermute | solution.py:42
  4.8 1.5 collective-permute-start
  6.4 0.7 add_convert_fusion.1
  7.1 6.6 %constant_dynamic-slice_fusion.12 = (bf16[3,512,512]{2,1,0:T(8,128)(2,1)S(1)}, bf16[3,512,512]{2,1,0:T(8,128)(2,1)S(1)}, bf16[3,512,512]{2,1,0:T(8,128)(2,1)S(1)...) fusion(bf16[3,4096,512]{2,1,0:T(8,128)(2,1)} %param.10, ...), kind=kLoop, calls=%fused_computation.143 | loop fusion | bytes 22020124 | tf_op jit(solution)/shard_map/dynamic_slice | solution.py:169
  13.7 4.8 %collective-permute-done = bf16[516,512]{1,0:T(8,128)(2,1)} collective-permute-done((bf16[516,512]{1,0:T(8,128)(2,1)S(1)}, bf16[516,512]{1,0:T(8,128)(2,1)}, u32[]{:S(2)}, u32[]{:S(2)}) %collective-permute-start) | collective-permute-done | bytes 528416 | tf_op jit(solution)/shard_map/ppermute | solution.py:42
  18.5 1.0 slice.258
  19.6 1.1 slice.255
  20.9 3.0 %collective-permute-start.4 = (bf16[516,512]{1,0:T(8,128)(2,1)S(1)}, bf16[516,512]{1,0:T(8,128)(2,1)S(1)}, u32[]{:S(2)}, u32[]{:S(2)}) collective-permute-start(bf16[516,512]{1,0:T(8,128)(2,1)S(1)} %get-tuple-element.46), channel_id=1, source_target_pairs={{0,6},{1,7},{2,0},{3,1},{4,2},{5,3},{6,4},{7,5},{8,14},{9,15},{10,... | collective-permute-start | bytes 1585160 | tf_op jit(solution)/shard_map/ppermute | solution.py:42
  23.9 1.5 collective-permute-start.3
  25.4 4.9 %fusion.2 = f32[3,512,516]{1,2,0:T(8,128)S(1)} fusion(bf16[3,512,512]{2,1,0:T(8,128)(2,1)S(1)} %get-tuple-element.10, bf16[3,512,512]{2,1,0:T(8,128)(2,1)S(1)} %get-tuple-element.11, bf16[3,512,512]{2,1,0:T(8,128)(2,1)S(1)} %copy-done.2, bf16[3,512,512]{2,1,0:T(8,128)(2,1)S(1)} %copy-done.3, bf16[516,512]{1,0:T(8,128)(2,1)} %collective-permute-done.2, ...), kind=kOutput, calls=%fused_computation.5 | convolution fusion | flops 3282124800 | bytes 11575296 | tf_op jit(solution)/shard_map/tn,cnf->ctf/dot_general | solution.py:177
  30.3 8.1 %collective-permute-done.5 = bf16[516,512]{1,0:T(8,128)(2,1)S(1)} collective-permute-done((bf16[516,512]{1,0:T(8,128)(2,1)S(1)}, bf16[516,512]{1,0:T(8,128)(2,1)S(1)}, u32[]{:S(2)}, u32[]{:S(2)}) %collective-permute-start.5) | collective-permute-done | bytes 528416 | tf_op jit(solution)/shard_map/ppermute | solution.py:42
  38.5 3.3 %collective-permute-start.7 = (bf16[516,128]{1,0:T(8,128)(2,1)S(1)}, bf16[516,128]{1,0:T(8,128)(2,1)S(1)}, u32[]{:S(2)}, u32[]{:S(2)}) collective-permute-start(bf16[516,128]{1,0:T(8,128)(2,1)S(1)} %slice.265), channel_id=1, source_target_pairs={{0,6},{1,7},{2,0},{3,1},{4,2},{5,3},{6,4},{7,5},{8,14},{9,15},{10,... | collective-permute-start | bytes 396296 | tf_op jit(solution)/shard_map/ppermute | solution.py:42
  41.9 0.8 collective-permute-start.6
  42.8 2.8 %fusion.10 = f32[3,512,516]{1,2,0:T(8,128)S(1)} fusion(bf16[3,512,512]{2,1,0:T(8,128)(2,1)S(1)} %get-tuple-element.14, bf16[3,512,512]{2,1,0:T(8,128)(2,1)S(1)} %get-tuple-element.9, bf16[3,512,512]{2,1,0:T(8,128)(2,1)S(1)} %get-tuple-element.8, bf16[516,1536]{1,0:T(8,128)(2,1)S(1)} %slice_dynamic-update-slice_fusion), kind=kOutput, calls=%fused_computation.13 | convolution fusion | flops 2448949248 | bytes 9474048 | tf_op jit(solution)/shard_map/tn,cnf->ctf/dot_general | solution.py:177
  45.6 3.0 %collective-permute-done.6 = bf16[516,256]{1,0:T(8,128)(2,1)S(1)} collective-permute-done((bf16[516,256]{1,0:T(8,128)(2,1)S(1)}, bf16[516,256]{1,0:T(8,128)(2,1)S(1)}, u32[]{:S(2)}, u32[]{:S(2)}) %collective-permute-start.6) | collective-permute-done | bytes 264224 | tf_op jit(solution)/shard_map/ppermute | solution.py:42
  48.6 2.7 %add_bitcast_fusion.proj_ref = f32[3,516,512]{2,1,0:T(8,128)S(1)} fusion(f32[3,512,516]{1,2,0:T(8,128)S(1)} %fusion.2, f32[3,512,516]{1,2,0:T(8,128)S(1)} %fusion.10, bf16[3,4096,512]{2,1,0:T(8,128)(2,1)} %param.10, s32[]{:T(128)S(6)} %select_n.114, bf16[516,128]{1,0:T(8,128)(2,1)S(1)} %collective-permute-done.8, ...), kind=kOutput, calls=%fused_computation.26 | convolution fusion | flops 814768128 | bytes 11612164 | tf_op jit(solution)/shard_map/tn,cnf->ctf/dot_general | solution.py:177
  51.7 0.6 collective-permute-start.9
  52.3 1.0 fusion.82
  53.3 2.1 %collective-permute-done.9 = f32[2,516]{1,0:T(2,128)S(1)} collective-permute-done((f32[2,516]{1,0:T(2,128)S(1)}, f32[2,516]{1,0:T(2,128)S(1)}, u32[]{:S(2)}, u32[]{:S(2)}) %collective-permute-start.9) | collective-permute-done | bytes 4160 | tf_op jit(solution)/shard_map/ppermute | solution.py:82
  55.5 1.0 pad_maximum_fusion.12
  56.5 2.6 %collective-permute-done.10 = f32[2,516]{1,0:T(2,128)S(1)} collective-permute-done((f32[2,516]{1,0:T(2,128)S(1)}, f32[2,516]{1,0:T(2,128)S(1)}, u32[]{:S(2)}, u32[]{:S(2)}) %collective-permute-start.10) | collective-permute-done | bytes 4160 | tf_op jit(solution)/shard_map/ppermute | solution.py:82
  59.2 0.6 broadcast_in_dim.43.gain_ref
  59.8 4.5 %collective-permute-done.11 = f32[2,516]{1,0:T(2,128)S(1)} collective-permute-done((f32[2,516]{1,0:T(2,128)S(1)}, f32[2,516]{1,0:T(2,128)S(1)}, u32[]{:S(2)}, u32[]{:S(2)}) %collective-permute-start.11) | collective-permute-done | bytes 4160 | tf_op jit(solution)/shard_map/ppermute | solution.py:82
  64.3 1.1 copy.10.square_ref
  65.4 4.1 %shard_map.95 = (bf16[16,3,128,128]{3,2,1,0:T(8,128)(2,1)}, f32[3,4,512]{2,1,0:T(4,128)}) custom-call(f32[3,516,512]{2,1,0:T(8,128)} %copy-done, f32[2,516,1]{2,1,0:T(8,128)} %copy.10.square_ref, f32[2,1,512]{2,1,0:T(1,128)} %broadcast_in_dim.43.gain_ref, f32[516,128]{1,0:T(8,128)} %get-tuple-element.61.cos_ref, f32[516,128]{1,0:T(8,128)} %get-tuple-element.62.sin_ref), custom_call_target="tpu_custom_call" | custom-call | tf_op jit(solution)/shard_map/pallas_call | solution.py:107
  69.5 7.7 %all-to-all-start = ((bf16[16,3,128,128]{3,2,1,0:T(8,128)(2,1)}), bf16[16,3,128,128]{3,2,1,0:T(8,128)(2,1)S(1)}, u32[]{:S(2)}, u32[]{:S(2)}) async-start(bf16[16,3,128,128]{3,2,1,0:T(8,128)(2,1)} %get-tuple-element.4), calls=%async_computation | async-start | bytes 3145728 | tf_op jit(solution)/shard_map/all_to_all | solution.py:206
  77.8 0.6 iota_compare_fusion.3
  78.4 0.7 iota_compare_fusion.2
  79.2 0.6 fusion.91
  80.4 16.8 %all-to-all-done = bf16[16,3,128,128]{3,2,1,0:T(8,128)(2,1)S(1)} async-done(((bf16[16,3,128,128]{3,2,1,0:T(8,128)(2,1)}), bf16[16,3,128,128]{3,2,1,0:T(8,128)(2,1)S(1)}, u32[]{:S(2)}, u32[]{:S(2)}) %all-to-all-start) | async-done | bytes 1572896 | tf_op jit(solution)/shard_map/all_to_all | solution.py:206
  97.6 1.3 fusion.83
  99.5 1.3 fusion.86
  100.8 0.9 fusion.109
  102.4 3.9 %fusion.1 = (f32[1024]{0:T(1024)S(1)}, f32[1024,2048]{1,0:T(8,128)S(1)}) fusion(s32[1024]{0:T(1024)S(1)} %iota_add_fusion, pred[2048]{0:T(1024)(128)(4,1)S(1)} %iota_compare_fusion.2, bf16[1024,128]{1,0:T(8,128)(2,1)} %bitcast.97, bf16[2048,128]{1,0:T(8,128)(2,1)S(1)} %bitcast.92), kind=kOutput, calls=%fused_computation.4 | convolution fusion | flops 547355648 | bytes 9185280 | tf_op jit(solution)/shard_map/dot_general | solution.py:125
  106.4 3.9 %fusion.106 = f32[1024]{0:T(1024)S(1)} fusion(f32[1024]{0:T(1024)S(1)} %get-tuple-element.53, f32[1024,2048]{1,0:T(8,128)S(1)} %get-tuple-element.54, pred[2048]{0:T(1024)(128)(4,1)S(1)} %iota_compare_fusion.2, s32[1024]{0:T(1024)S(1)} %iota_add_fusion), kind=kLoop, calls=%fused_computation.177 | loop fusion | flops 14679040 | bytes 8402944 | tf_op jit(solution)/shard_map/reduce_sum | solution.py:134
  110.3 3.6 %fusion.55 = bf16[1024,128]{1,0:T(8,128)(2,1)S(1)} fusion(bf16[2048,128]{1,0:T(8,128)(2,1)S(1)} %bitcast.89, f32[1024]{0:T(1024)S(1)} %fusion.106, f32[1024,2048]{1,0:T(8,128)S(1)} %get-tuple-element.54, f32[1024]{0:T(1024)S(1)} %get-tuple-element.53, s32[1024]{0:T(1024)S(1)} %iota_add_fusion, pred[2048]{0:T(1024)(128)(4,1)S(1)} %iota_compare_fusion.2), kind=kOutput, calls=%fused_computation.58 | convolution fusion | flops 551813120 | bytes 9189376 | tf_op jit(solution)/shard_map/dot_general | solution.py:136
  113.9 1.6 fusion.19
  115.5 2.1 %fusion.68 = f32[1024]{0:T(1024)S(1)} fusion(f32[1024]{0:T(1024)S(1)} %get-tuple-element.55, f32[1024,1024]{0,1:T(8,128)S(1)} %get-tuple-element.56, pred[1024]{0:T(1024)(128)(4,1)S(1)} %iota_compare_fusion.3), kind=kLoop, calls=%fused_computation.73 | loop fusion | flops 7339008 | bytes 4203520 | tf_op jit(solution)/shard_map/reduce_sum | solution.py:134
  117.7 1.1 fusion.58
  119.0 0.9 pad_maximum_fusion.2
  119.9 8.0 %all-to-all-start.1 = ((bf16[16,136,128]{2,1,0:T(8,128)(2,1)}), bf16[16,136,128]{2,1,0:T(8,128)(2,1)S(1)}, u32[]{:S(2)}, u32[]{:S(2)}) async-start(bf16[16,136,128]{2,1,0:T(8,128)(2,1)} %pad_maximum_fusion.2), calls=%async_computation.1 | async-start | bytes 1114112 | tf_op jit(solution)/shard_map/all_to_all | solution.py:221
  127.9 3.3 %constant_dynamic-slice_fusion.6 = (bf16[512,512]{1,0:T(8,128)(2,1)S(1)}, bf16[512,512]{1,0:T(8,128)(2,1)S(1)}, bf16[512,512]{1,0:T(8,128)(2,1)S(1)}, bf16[512,5...) fusion(bf16[512,4096]{1,0:T(8,128)(2,1)} %param.11, ...), kind=kLoop, calls=%fused_computation.136 | loop fusion | bytes 7340060 | tf_op jit(solution)/shard_map/dynamic_slice | solution.py:169
  131.2 5.8 %all-to-all-done.1 = bf16[16,136,128]{2,1,0:T(8,128)(2,1)S(1)} async-done(((bf16[16,136,128]{2,1,0:T(8,128)(2,1)}), bf16[16,136,128]{2,1,0:T(8,128)(2,1)S(1)}, u32[]{:S(2)}, u32[]{:S(2)}) %all-to-all-start.1) | async-done | bytes 557088 | tf_op jit(solution)/shard_map/all_to_all | solution.py:221
  137.5 1.5 convolution_convert_fusion
  139.1 3.2 %collective-permute-start.15 = (bf16[516,128]{1,0:T(8,128)(2,1)S(1)}, bf16[516,128]{1,0:T(8,128)(2,1)S(1)}, u32[]{:S(2)}, u32[]{:S(2)}) collective-permute-start(bf16[516,128]{1,0:T(8,128)(2,1)S(1)} %get-tuple-element.40), channel_id=1, source_target_pairs={{0,6},{1,7},{2,0},{3,1},{4,2},{5,3},{6,4},{7,5},{8,14},{9,15},{10,... | collective-permute-start | bytes 396296 | tf_op jit(solution)/shard_map/ppermute | solution.py:62
  142.4 1.0 fusion.114
  143.9 2.1 %collective-permute-start.18 = (bf16[516,512]{1,0:T(8,128)(2,1)S(1)}, bf16[516,512]{1,0:T(8,128)(2,1)S(1)}, u32[]{:S(2)}, u32[]{:S(2)}) collective-permute-start(bf16[516,512]{1,0:T(8,128)(2,1)S(1)} %pad_maximum_fusion.8), channel_id=1, source_target_pairs={{0,1},{1,0},{2,3},{3,2},{4,5},{5,4},{6,7},{7,6},{8,9},{9,8},{10,11... | collective-permute-start | bytes 1585160 | tf_op jit(solution)/shard_map/ppermute | solution.py:62
  146.7 3.0 %collective-permute-start.16 = (bf16[516,512]{1,0:T(8,128)(2,1)S(1)}, bf16[516,512]{1,0:T(8,128)(2,1)S(1)}, u32[]{:S(2)}, u32[]{:S(2)}) collective-permute-start(bf16[516,512]{1,0:T(8,128)(2,1)S(1)} %fusion.73), channel_id=1, source_target_pairs={{0,6},{1,7},{2,0},{3,1},{4,2},{5,3},{6,4},{7,5},{8,14},{9,15},{10,... | collective-permute-start | bytes 1585160 | tf_op jit(solution)/shard_map/ppermute | solution.py:62
  149.7 3.4 %collective-permute-done.13 = bf16[516,256]{1,0:T(8,128)(2,1)S(1)} collective-permute-done((bf16[516,256]{1,0:T(8,128)(2,1)S(1)}, bf16[516,256]{1,0:T(8,128)(2,1)S(1)}, u32[]{:S(2)}, u32[]{:S(2)}) %collective-permute-start.13) | collective-permute-done | bytes 264224 | tf_op jit(solution)/shard_map/ppermute | solution.py:62
  153.4 1.3 fusion.115
  154.7 9.1 %collective-permute-done.18 = bf16[516,512]{1,0:T(8,128)(2,1)S(1)} collective-permute-done((bf16[516,512]{1,0:T(8,128)(2,1)S(1)}, bf16[516,512]{1,0:T(8,128)(2,1)S(1)}, u32[]{:S(2)}, u32[]{:S(2)}) %collective-permute-start.18) | collective-permute-done | bytes 528416 | tf_op jit(solution)/shard_map/ppermute | solution.py:62
  164.1 3.1 %collective-permute-done.14 = bf16[516,512]{1,0:T(8,128)(2,1)S(1)} collective-permute-done((bf16[516,512]{1,0:T(8,128)(2,1)S(1)}, bf16[516,512]{1,0:T(8,128)(2,1)S(1)}, u32[]{:S(2)}, u32[]{:S(2)}) %collective-permute-start.14) | collective-permute-done | bytes 528416 | tf_op jit(solution)/shard_map/ppermute | solution.py:62
  168.1 2.1 %collective-permute-start.19 = (bf16[516,512]{1,0:T(8,128)(2,1)S(1)}, bf16[516,512]{1,0:T(8,128)(2,1)S(1)}, u32[]{:S(2)}, u32[]{:S(2)}) collective-permute-start(bf16[516,512]{1,0:T(8,128)(2,1)S(1)} %pad_maximum_fusion.9), channel_id=1, source_target_pairs={{0,2},{1,3},{2,4},{3,5},{4,6},{5,7},{6,0},{7,1},{8,10},{9,11},{10,... | collective-permute-start | bytes 1585160 | tf_op jit(solution)/shard_map/ppermute | solution.py:62
  170.2 0.7 collective-permute-start.17
  170.9 8.9 %collective-permute-done.20 = bf16[516,512]{1,0:T(8,128)(2,1)S(1)} collective-permute-done((bf16[516,512]{1,0:T(8,128)(2,1)S(1)}, bf16[516,512]{1,0:T(8,128)(2,1)S(1)}, u32[]{:S(2)}, u32[]{:S(2)}) %collective-permute-start.20) | collective-permute-done | bytes 528416 | tf_op jit(solution)/shard_map/ppermute | solution.py:62
  179.8 1.3 collective-permute-done.19
  181.9 1.3 collective-permute-start.21
  183.1 2.4 %collective-permute-done.21 = f32[516]{0:T(1024)S(1)} collective-permute-done((f32[516]{0:T(1024)S(1)}, f32[516]{0:T(1024)S(1)}, u32[]{:S(2)}, u32[]{:S(2)}) %collective-permute-start.21) | collective-permute-done | bytes 2096 | tf_op jit(solution)/shard_map/ppermute | solution.py:82
  185.9 3.3 %collective-permute-done.22 = f32[516]{0:T(1024)S(1)} collective-permute-done((f32[516]{0:T(1024)S(1)}, f32[516]{0:T(1024)S(1)}, u32[]{:S(2)}, u32[]{:S(2)}) %collective-permute-start.22) | collective-permute-done | bytes 2096 | tf_op jit(solution)/shard_map/ppermute | solution.py:82
  189.2 0.9 collective-permute-start.23
  190.1 4.2 %collective-permute-done.23 = f32[516]{0:T(1024)S(1)} collective-permute-done((f32[516]{0:T(1024)S(1)}, f32[516]{0:T(1024)S(1)}, u32[]{:S(2)}, u32[]{:S(2)}) %collective-permute-start.23) | collective-permute-done | bytes 2096 | tf_op jit(solution)/shard_map/ppermute | solution.py:82
  194.7 0.8 slice.301
  195.5 0.6 slice.302
  (110 shorter events, 6.9 us)
Async XLA Ops:
  1.7 17.9 %collective-permute-start.2 = (bf16[516,512]{1,0:T(8,128)(2,1)S(1)}, bf16[516,512]{1,0:T(8,128)(2,1)}, u32[]{:S(2)}, u32[]{:S(2)}) collective-permute-start(bf16[516,512]{1,0:T(8,128)(2,1)S(1)} %pad_maximum_fusion.4), channel_id=1, source_target_pairs={{0,6},{1,7},{2,0},{3,1},{4,2},{5,3},{6,4},{7,5},{8,14},{9,15},{10,... | collective-permute-start | bytes 1585160 | tf_op jit(solution)/shard_map/ppermute | solution.py:42
  4.8 14.8 %collective-permute-start.1 = (bf16[516,512]{1,0:T(8,128)(2,1)S(1)}, bf16[516,512]{1,0:T(8,128)(2,1)S(1)}, u32[]{:S(2)}, u32[]{:S(2)}) collective-permute-start(bf16[516,512]{1,0:T(8,128)(2,1)S(1)} %pad_maximum_fusion.4), channel_id=1, source_target_pairs={{0,2},{1,3},{2,4},{3,5},{4,6},{5,7},{6,0},{7,1},{8,10},{9,11},{10,... | collective-permute-start | bytes 1585160 | tf_op jit(solution)/shard_map/ppermute | solution.py:42
  4.8 13.7 %collective-permute-start = (bf16[516,512]{1,0:T(8,128)(2,1)S(1)}, bf16[516,512]{1,0:T(8,128)(2,1)}, u32[]{:S(2)}, u32[]{:S(2)}) collective-permute-start(bf16[516,512]{1,0:T(8,128)(2,1)S(1)} %pad_maximum_fusion.4), channel_id=1, source_target_pairs={{0,1},{1,0},{2,3},{3,2},{4,5},{5,4},{6,7},{7,6},{8,9},{9,8},{10,11... | collective-permute-start | bytes 1585160 | tf_op jit(solution)/shard_map/ppermute | solution.py:42
  19.5 5.9 %copy-start.1 = (bf16[4,128,512]{2,1,0:T(8,128)(2,1)S(1)}, bf16[4,128,512]{2,1,0:T(8,128)(2,1)}, u32[]{:S(2)}) copy-start(bf16[4,128,512]{2,1,0:T(8,128)(2,1)} %param.8) | copy-start | bytes 1572868
  19.5 5.9 %copy-start.2 = (bf16[3,512,512]{2,1,0:T(8,128)(2,1)S(1)}, bf16[3,512,512]{2,1,0:T(8,128)(2,1)}, u32[]{:S(2)}) copy-start(bf16[3,512,512]{2,1,0:T(8,128)(2,1)} %get-tuple-element.12) | copy-start | bytes 4718596
  19.5 5.9 %copy-start.3 = (bf16[3,512,512]{2,1,0:T(8,128)(2,1)S(1)}, bf16[3,512,512]{2,1,0:T(8,128)(2,1)}, u32[]{:S(2)}) copy-start(bf16[3,512,512]{2,1,0:T(8,128)(2,1)} %get-tuple-element.13) | copy-start | bytes 4718596
  19.5 5.9 %copy-start.10 = (bf16[4,512]{1,0:T(4,128)(2,1)S(1)}, bf16[4,512]{1,0:T(4,128)(2,1)}, u32[]{:S(2)}) copy-start(bf16[4,512]{1,0:T(4,128)(2,1)} %param.9) | copy-start | bytes 12292
  20.9 17.6 %collective-permute-start.4 = (bf16[516,512]{1,0:T(8,128)(2,1)S(1)}, bf16[516,512]{1,0:T(8,128)(2,1)S(1)}, u32[]{:S(2)}, u32[]{:S(2)}) collective-permute-start(bf16[516,512]{1,0:T(8,128)(2,1)S(1)} %get-tuple-element.46), channel_id=1, source_target_pairs={{0,6},{1,7},{2,0},{3,1},{4,2},{5,3},{6,4},{7,5},{8,14},{9,15},{10,... | collective-permute-start | bytes 1585160 | tf_op jit(solution)/shard_map/ppermute | solution.py:42
  23.9 17.9 %collective-permute-start.3 = (bf16[516,512]{1,0:T(8,128)(2,1)S(1)}, bf16[516,512]{1,0:T(8,128)(2,1)S(1)}, u32[]{:S(2)}, u32[]{:S(2)}) collective-permute-start(bf16[516,512]{1,0:T(8,128)(2,1)S(1)} %get-tuple-element.47), channel_id=1, source_target_pairs={{0,1},{1,0},{2,3},{3,2},{4,5},{5,4},{6,7},{7,6},{8,9},{9,8},{10,11... | collective-permute-start | bytes 1585160 | tf_op jit(solution)/shard_map/ppermute | solution.py:42
  25.4 13.0 %collective-permute-start.5 = (bf16[516,512]{1,0:T(8,128)(2,1)S(1)}, bf16[516,512]{1,0:T(8,128)(2,1)S(1)}, u32[]{:S(2)}, u32[]{:S(2)}) collective-permute-start(bf16[516,512]{1,0:T(8,128)(2,1)S(1)} %get-tuple-element.45), channel_id=1, source_target_pairs={{0,2},{1,3},{2,4},{3,5},{4,6},{5,7},{6,0},{7,1},{8,10},{9,11},{10,... | collective-permute-start | bytes 1585160 | tf_op jit(solution)/shard_map/ppermute | solution.py:42
  38.4 7.2 %collective-permute-start.8 = (bf16[516,128]{1,0:T(8,128)(2,1)S(1)}, bf16[516,128]{1,0:T(8,128)(2,1)S(1)}, u32[]{:S(2)}, u32[]{:S(2)}) collective-permute-start(bf16[516,128]{1,0:T(8,128)(2,1)S(1)} %slice.266), channel_id=1, source_target_pairs={{0,2},{1,3},{2,4},{3,5},{4,6},{5,7},{6,0},{7,1},{8,10},{9,11},{10,... | collective-permute-start | bytes 396296 | tf_op jit(solution)/shard_map/ppermute | solution.py:42
  38.5 7.1 %collective-permute-start.7 = (bf16[516,128]{1,0:T(8,128)(2,1)S(1)}, bf16[516,128]{1,0:T(8,128)(2,1)S(1)}, u32[]{:S(2)}, u32[]{:S(2)}) collective-permute-start(bf16[516,128]{1,0:T(8,128)(2,1)S(1)} %slice.265), channel_id=1, source_target_pairs={{0,6},{1,7},{2,0},{3,1},{4,2},{5,3},{6,4},{7,5},{8,14},{9,15},{10,... | collective-permute-start | bytes 396296 | tf_op jit(solution)/shard_map/ppermute | solution.py:42
  41.9 6.7 %collective-permute-start.6 = (bf16[516,256]{1,0:T(8,128)(2,1)S(1)}, bf16[516,256]{1,0:T(8,128)(2,1)S(1)}, u32[]{:S(2)}, u32[]{:S(2)}) collective-permute-start(bf16[516,256]{1,0:T(8,128)(2,1)S(1)} %get-tuple-element.41), channel_id=1, source_target_pairs={{0,1},{1,0},{2,3},{3,2},{4,5},{5,4},{6,7},{7,6},{8,9},{9,8},{10,11... | collective-permute-start | bytes 792584 | tf_op jit(solution)/shard_map/ppermute | solution.py:42
  51.3 5.1 %copy-start = (f32[3,516,512]{2,1,0:T(8,128)}, f32[3,516,512]{2,1,0:T(8,128)S(1)}, u32[]{:S(2)}) copy-start(f32[3,516,512]{2,1,0:T(8,128)S(1)} %add_bitcast_fusion.proj_ref) | copy-start | bytes 9510916
  51.3 7.8 %copy-start.12 = (f32[512]{0:T(512)S(1)}, f32[512]{0:T(512)}, u32[]{:S(2)}) copy-start(f32[512]{0:T(512)} %param.13) | copy-start | bytes 6148
  51.4 7.8 %copy-start.13 = (f32[512]{0:T(512)S(1)}, f32[512]{0:T(512)}, u32[]{:S(2)}) copy-start(f32[512]{0:T(512)} %param.12) | copy-start | bytes 6148
  51.7 3.7 %collective-permute-start.9 = (f32[2,516]{1,0:T(2,128)S(1)}, f32[2,516]{1,0:T(2,128)S(1)}, u32[]{:S(2)}, u32[]{:S(2)}) collective-permute-start(f32[2,516]{1,0:T(2,128)S(1)} %pad_maximum_fusion.14), channel_id=1, source_target_pairs={{0,1},{1,0},{2,3},{3,2},{4,5},{5,4},{6,7},{7,6},{8,9},{9,8},{10,11... | collective-permute-start | bytes 12392 | tf_op jit(solution)/shard_map/ppermute | solution.py:82
  55.4 3.7 %collective-permute-start.10 = (f32[2,516]{1,0:T(2,128)S(1)}, f32[2,516]{1,0:T(2,128)S(1)}, u32[]{:S(2)}, u32[]{:S(2)}) collective-permute-start(f32[2,516]{1,0:T(2,128)S(1)} %fusion.105), channel_id=1, source_target_pairs={{0,2},{1,3},{2,0},{3,1},{4,6},{5,7},{6,4},{7,5},{8,10},{9,11},{10,... | collective-permute-start | bytes 12392 | tf_op jit(solution)/shard_map/ppermute | solution.py:82
  59.1 5.2 %collective-permute-start.11 = (f32[2,516]{1,0:T(2,128)S(1)}, f32[2,516]{1,0:T(2,128)S(1)}, u32[]{:S(2)}, u32[]{:S(2)}) collective-permute-start(f32[2,516]{1,0:T(2,128)S(1)} %fusion.128), channel_id=1, source_target_pairs={{0,4},{1,5},{2,6},{3,7},{4,0},{5,1},{6,2},{7,3},{8,12},{9,13},{10,... | collective-permute-start | bytes 12392 | tf_op jit(solution)/shard_map/ppermute | solution.py:82
  69.5 7.7 %copy-start.14 = (s32[4]{0:T(128)S(1)}, s32[4]{0:T(128)}, u32[]{:S(2)}) copy-start(s32[4]{0:T(128)} %param.15) | copy-start | bytes 52
  69.5 9.7 %copy-start.9 = (f32[3,4,512]{2,1,0:T(4,128)S(1)}, f32[3,4,512]{2,1,0:T(4,128)}, u32[]{:S(2)}) copy-start(f32[3,4,512]{2,1,0:T(4,128)} %get-tuple-element.5) | copy-start | bytes 73732
  69.5 27.8 %all-to-all-start = ((bf16[16,3,128,128]{3,2,1,0:T(8,128)(2,1)}), bf16[16,3,128,128]{3,2,1,0:T(8,128)(2,1)S(1)}, u32[]{:S(2)}, u32[]{:S(2)}) async-start(bf16[16,3,128,128]{3,2,1,0:T(8,128)(2,1)} %get-tuple-element.4), calls=%async_computation | async-start | bytes 3145728 | tf_op jit(solution)/shard_map/all_to_all | solution.py:206
  110.3 3.6 %copy-start.7 = (bf16[1,8,128,128]{3,2,0,1:T(8,128)(2,1)S(1)}, bf16[1,8,128,128]{3,2,0,1:T(8,128)(2,1)}, u32[]{:S(2)}) copy-start(bf16[1,8,128,128]{3,2,0,1:T(8,128)(2,1)} %get-tuple-element.33) | copy-start | bytes 786436
  110.3 3.6 %copy-start.8 = (bf16[1,8,128,128]{3,2,0,1:T(8,128)(2,1)S(1)}, bf16[1,8,128,128]{3,2,0,1:T(8,128)(2,1)}, u32[]{:S(2)}) copy-start(bf16[1,8,128,128]{3,2,0,1:T(8,128)(2,1)} %get-tuple-element.36) | copy-start | bytes 786436
  119.9 17.1 %all-to-all-start.1 = ((bf16[16,136,128]{2,1,0:T(8,128)(2,1)}), bf16[16,136,128]{2,1,0:T(8,128)(2,1)S(1)}, u32[]{:S(2)}, u32[]{:S(2)}) async-start(bf16[16,136,128]{2,1,0:T(8,128)(2,1)} %pad_maximum_fusion.2), calls=%async_computation.1 | async-start | bytes 1114112 | tf_op jit(solution)/shard_map/all_to_all | solution.py:221
  139.1 7.5 %collective-permute-start.12 = (bf16[516,128]{1,0:T(8,128)(2,1)S(1)}, bf16[516,128]{1,0:T(8,128)(2,1)S(1)}, u32[]{:S(2)}, u32[]{:S(2)}) collective-permute-start(bf16[516,128]{1,0:T(8,128)(2,1)S(1)} %get-tuple-element.39), channel_id=1, source_target_pairs={{0,2},{1,3},{2,4},{3,5},{4,6},{5,7},{6,0},{7,1},{8,10},{9,11},{10,... | collective-permute-start | bytes 396296 | tf_op jit(solution)/shard_map/ppermute | solution.py:62
  139.1 7.4 %collective-permute-start.15 = (bf16[516,128]{1,0:T(8,128)(2,1)S(1)}, bf16[516,128]{1,0:T(8,128)(2,1)S(1)}, u32[]{:S(2)}, u32[]{:S(2)}) collective-permute-start(bf16[516,128]{1,0:T(8,128)(2,1)S(1)} %get-tuple-element.40), channel_id=1, source_target_pairs={{0,6},{1,7},{2,0},{3,1},{4,2},{5,3},{6,4},{7,5},{8,14},{9,15},{10,... | collective-permute-start | bytes 396296 | tf_op jit(solution)/shard_map/ppermute | solution.py:62
  143.5 9.6 %collective-permute-start.13 = (bf16[516,256]{1,0:T(8,128)(2,1)S(1)}, bf16[516,256]{1,0:T(8,128)(2,1)S(1)}, u32[]{:S(2)}, u32[]{:S(2)}) collective-permute-start(bf16[516,256]{1,0:T(8,128)(2,1)S(1)} %slice.284), channel_id=1, source_target_pairs={{0,1},{1,0},{2,3},{3,2},{4,5},{5,4},{6,7},{7,6},{8,9},{9,8},{10,11... | collective-permute-start | bytes 792584 | tf_op jit(solution)/shard_map/ppermute | solution.py:62
  143.9 19.9 %collective-permute-start.18 = (bf16[516,512]{1,0:T(8,128)(2,1)S(1)}, bf16[516,512]{1,0:T(8,128)(2,1)S(1)}, u32[]{:S(2)}, u32[]{:S(2)}) collective-permute-start(bf16[516,512]{1,0:T(8,128)(2,1)S(1)} %pad_maximum_fusion.8), channel_id=1, source_target_pairs={{0,1},{1,0},{2,3},{3,2},{4,5},{5,4},{6,7},{7,6},{8,9},{9,8},{10,11... | collective-permute-start | bytes 1585160 | tf_op jit(solution)/shard_map/ppermute | solution.py:62
  146.6 6.8 %copy-start.4 = (bf16[512,512]{1,0:T(8,128)(2,1)S(1)}, bf16[512,512]{1,0:T(8,128)(2,1)}, u32[]{:S(2)}) copy-start(bf16[512,512]{1,0:T(8,128)(2,1)} %get-tuple-element.22) | copy-start | bytes 1572868
  146.6 6.8 %copy-start.5 = (bf16[512,512]{1,0:T(8,128)(2,1)S(1)}, bf16[512,512]{1,0:T(8,128)(2,1)}, u32[]{:S(2)}) copy-start(bf16[512,512]{1,0:T(8,128)(2,1)} %get-tuple-element.23) | copy-start | bytes 1572868
  146.6 6.8 %copy-start.6 = (bf16[512,512]{1,0:T(8,128)(2,1)S(1)}, bf16[512,512]{1,0:T(8,128)(2,1)}, u32[]{:S(2)}) copy-start(bf16[512,512]{1,0:T(8,128)(2,1)} %get-tuple-element.24) | copy-start | bytes 1572868
  146.7 17.2 %collective-permute-start.16 = (bf16[516,512]{1,0:T(8,128)(2,1)S(1)}, bf16[516,512]{1,0:T(8,128)(2,1)S(1)}, u32[]{:S(2)}, u32[]{:S(2)}) collective-permute-start(bf16[516,512]{1,0:T(8,128)(2,1)S(1)} %fusion.73), channel_id=1, source_target_pairs={{0,6},{1,7},{2,0},{3,1},{4,2},{5,3},{6,4},{7,5},{8,14},{9,15},{10,... | collective-permute-start | bytes 1585160 | tf_op jit(solution)/shard_map/ppermute | solution.py:62
  153.3 14.0 %collective-permute-start.14 = (bf16[516,512]{1,0:T(8,128)(2,1)S(1)}, bf16[516,512]{1,0:T(8,128)(2,1)S(1)}, u32[]{:S(2)}, u32[]{:S(2)}) collective-permute-start(bf16[516,512]{1,0:T(8,128)(2,1)S(1)} %pad_maximum_fusion.6), channel_id=1, source_target_pairs={{0,2},{1,3},{2,4},{3,5},{4,6},{5,7},{6,0},{7,1},{8,10},{9,11},{10,... | collective-permute-start | bytes 1585160 | tf_op jit(solution)/shard_map/ppermute | solution.py:62
  167.9 11.8 %collective-permute-start.20 = (bf16[516,512]{1,0:T(8,128)(2,1)S(1)}, bf16[516,512]{1,0:T(8,128)(2,1)S(1)}, u32[]{:S(2)}, u32[]{:S(2)}) collective-permute-start(bf16[516,512]{1,0:T(8,128)(2,1)S(1)} %pad_maximum_fusion.10), channel_id=1, source_target_pairs={{0,6},{1,7},{2,0},{3,1},{4,2},{5,3},{6,4},{7,5},{8,14},{9,15},{10,... | collective-permute-start | bytes 1585160 | tf_op jit(solution)/shard_map/ppermute | solution.py:62
  168.1 26.2 %copy-start.11 = (f32[512]{0:T(512)S(1)}, f32[512]{0:T(512)}, u32[]{:S(2)}) copy-start(f32[512]{0:T(512)} %param.14) | copy-start | bytes 6148
  168.1 13.0 %collective-permute-start.19 = (bf16[516,512]{1,0:T(8,128)(2,1)S(1)}, bf16[516,512]{1,0:T(8,128)(2,1)S(1)}, u32[]{:S(2)}, u32[]{:S(2)}) collective-permute-start(bf16[516,512]{1,0:T(8,128)(2,1)S(1)} %pad_maximum_fusion.9), channel_id=1, source_target_pairs={{0,2},{1,3},{2,4},{3,5},{4,6},{5,7},{6,0},{7,1},{8,10},{9,11},{10,... | collective-permute-start | bytes 1585160 | tf_op jit(solution)/shard_map/ppermute | solution.py:62
  170.2 11.3 %collective-permute-start.17 = (bf16[516,512]{1,0:T(8,128)(2,1)S(1)}, bf16[516,512]{1,0:T(8,128)(2,1)S(1)}, u32[]{:S(2)}, u32[]{:S(2)}) collective-permute-start(bf16[516,512]{1,0:T(8,128)(2,1)S(1)} %pad_maximum_fusion.7), channel_id=1, source_target_pairs={{0,1},{1,0},{2,3},{3,2},{4,5},{5,4},{6,7},{7,6},{8,9},{9,8},{10,11... | collective-permute-start | bytes 1585160 | tf_op jit(solution)/shard_map/ppermute | solution.py:62
  181.9 3.7 %collective-permute-start.21 = (f32[516]{0:T(1024)S(1)}, f32[516]{0:T(1024)S(1)}, u32[]{:S(2)}, u32[]{:S(2)}) collective-permute-start(f32[516]{0:T(1024)S(1)} %multiply_reduce_fusion), channel_id=1, source_target_pairs={{0,1},{1,0},{2,3},{3,2},{4,5},{5,4},{6,7},{7,6},{8,9},{9,8},{10,11... | collective-permute-start | bytes 6200 | tf_op jit(solution)/shard_map/ppermute | solution.py:82
  185.6 3.6 %collective-permute-start.22 = (f32[516]{0:T(1024)S(1)}, f32[516]{0:T(1024)S(1)}, u32[]{:S(2)}, u32[]{:S(2)}) collective-permute-start(f32[516]{0:T(1024)S(1)} %add.248), channel_id=1, source_target_pairs={{0,2},{1,3},{2,0},{3,1},{4,6},{5,7},{6,4},{7,5},{8,10},{9,11},{10,... | collective-permute-start | bytes 6200 | tf_op jit(solution)/shard_map/ppermute | solution.py:82
  189.2 5.1 %collective-permute-start.23 = (f32[516]{0:T(1024)S(1)}, f32[516]{0:T(1024)S(1)}, u32[]{:S(2)}, u32[]{:S(2)}) collective-permute-start(f32[516]{0:T(1024)S(1)} %add.249), channel_id=1, source_target_pairs={{0,4},{1,5},{2,6},{3,7},{4,0},{5,1},{6,2},{7,3},{8,12},{9,13},{10,... | collective-permute-start | bytes 6200 | tf_op jit(solution)/shard_map/ppermute | solution.py:82

commit v2 on v1

--- a/solution.py
+++ b/solution.py
@@ -116,16 +116,14 @@
 def attend_pair(q_all, k_all, v_all, q_new, k_new, v_new, length):
     count = q_all.shape[0]
     scale = HD ** (-0.5)
-    chunks = 2
-    size = count // chunks
+    bounds = (0, count // 4, count // 2, count * 3 // 4, count)
     outs = []
-    for c in range(chunks):
-        stop = (c + 1) * size
+    for begin, stop in zip(bounds[:-1], bounds[1:]):
         scores = (
-            jnp.dot(q_all[c * size:stop], k_all[:stop].T, preferred_element_type=jnp.float32)
+            jnp.dot(q_all[begin:stop], k_all[:stop].T, preferred_element_type=jnp.float32)
             * scale
         )
-        query_pos = c * size + jnp.arange(size, dtype=jnp.int32)[:, None]
+        query_pos = begin + jnp.arange(stop - begin, dtype=jnp.int32)[:, None]
         key_pos = jnp.arange(stop, dtype=jnp.int32)[None, :]
         valid = (key_pos <= query_pos) & (key_pos < length)
         scores = jnp.where(valid, scores, masked_fill)

time: 197 us -> 195 us (0.990)
  waiting for transfers between devices: 84.4 us -> 79.1 us
  other arithmetic: 17.8 us -> 21.3 us
  matrix products: 24.8 us -> 22.7 us
  local copies, waits for them, and re-layouts: 17.7 us -> 19.8 us
    all_to_all x1, waiting for transfers between devices: 16.8 us -> 11.6 us  [body(): got = lax.all_to_all(qkv, 'seq', 0, 0, tiled=True)]
    lt x2 -> x4, other arithmetic: 1.3 us -> 4.83 us  [attend_pair(): valid = (key_pos <= query_pos) & (key_pos < length)]
    reduce_sum x2 -> x4, other arithmetic: 6.03 us -> 3.69 us  [attend_pair(): total = jnp.sum(weights, -1, keepdims=True)]
    dot_general x2 -> x4, matrix products: 4.69 us -> 3.55 us  [attend_pair(): jnp.dot(weights.astype(jnp.bfloat16), v_all[:stop], preferred_element_typ...]
    dot_general x2 -> x4, matrix products: 5.53 us -> 4.5 us  [attend_pair(): jnp.dot(q_all[begin:stop], k_all[:stop].T, preferred_element_type=jnp.flo...]
  transfers between devices with their start and end apart: 26 -> 26, of which waited for: 19 -> 19; matrix products, arithmetic and copies ran while one was open for 14% -> 17% of each run, Pallas kernels for 0% -> 0%
where the time goes in v2:
time: 195 us; the launch traced here: 194 us
  waiting for transfers between devices  79.1 us (41%)
  starting transfers between devices  43.6 us (22%)
  matrix products  22.7 us (12%)
  other arithmetic  21.3 us (11%)
  local copies, waits for them, and re-layouts  19.8 us (10%)
  Pallas kernels  4.1 us (2%)
  between operations  3.58 us (2%)
    ppermute x9, waiting for transfers between devices, tp_reduce_scatter(): lax.ppermute(value.astype(jnp.bfloat16), 'tp', perm).astype(jnp.float32)  26.8 us
    ppermute x6, waiting for transfers between devices, tp_sum(): lax.ppermute(v, 'tp', [(i, i ^ bit) for i in range(8)])  19 us
    ppermute x9, waiting for transfers between devices, tp_gather(): send = lambda value, perm: lax.ppermute(value, 'tp', perm)  16 us
    ppermute x9, starting transfers between devices, tp_gather(): send = lambda value, perm: lax.ppermute(value, 'tp', perm)  13.2 us
    all_to_all x1, waiting for transfers between devices, body(): got = lax.all_to_all(qkv, 'seq', 0, 0, tiled=True)  11.6 us
    ppermute x9, starting transfers between devices, tp_reduce_scatter(): lax.ppermute(value.astype(jnp.bfloat16), 'tp', perm).astype(jnp.float32)  11.4 us
    dot_general x3, matrix products, body(): jnp.einsum('tn,cnf->ctf', jnp.concatenate(blocks, 1), jnp.concatenate(w_b...  10.4 us
    dynamic_slice x2, local copies, waits for them, and re-layouts, in_relative_order(): lax.dynamic_slice_in_dim(weight, order[name] * width_local, width_local,...  9.87 us
  transfers between devices with their start and end apart: 26, of which 19 were waited for; matrix products, arithmetic and copies ran while one was open for 17% of the time, Pallas kernels for 0%

profile of v2, /device:TPU:32, one launch (start us, length us, event | category | flops | bytes accessed | tf_op | source)
XLA Modules:
  0.0 194.2 jit_solution(2890171862921041302)
XLA Ops:
  0.6 1.1 pad_maximum_fusion.4
  1.7 3.1 %collective-permute-start.2 = (bf16[516,512]{1,0:T(8,128)(2,1)S(1)}, bf16[516,512]{1,0:T(8,128)(2,1)}, u32[]{:S(2)}, u32[]{:S(2)}) collective-permute-start(bf16[516,512]{1,0:T(8,128)(2,1)S(1)} %pad_maximum_fusion.4), channel_id=1, source_target_pairs={{0,6},{1,7},{2,0},{3,1},{4,2},{5,3},{6,4},{7,5},{8,14},{9,15},{10,... | collective-permute-start | bytes 1585160 | tf_op jit(solution)/shard_map/ppermute | solution.py:42
  4.8 1.5 collective-permute-start
  7.1 6.5 %constant_dynamic-slice_fusion.12 = (bf16[3,512,512]{2,1,0:T(8,128)(2,1)S(1)}, bf16[3,512,512]{2,1,0:T(8,128)(2,1)S(1)}, bf16[3,512,512]{2,1,0:T(8,128)(2,1)S(1)...) fusion(bf16[3,4096,512]{2,1,0:T(8,128)(2,1)} %param.10, ...), kind=kLoop, calls=%fused_computation.167 | loop fusion | bytes 22020124 | tf_op jit(solution)/shard_map/dynamic_slice | solution.py:167
  13.6 4.8 %collective-permute-done = bf16[516,512]{1,0:T(8,128)(2,1)} collective-permute-done((bf16[516,512]{1,0:T(8,128)(2,1)S(1)}, bf16[516,512]{1,0:T(8,128)(2,1)}, u32[]{:S(2)}, u32[]{:S(2)}) %collective-permute-start) | collective-permute-done | bytes 528416 | tf_op jit(solution)/shard_map/ppermute | solution.py:42
  18.5 1.0 slice.312
  19.6 1.1 slice.309
  20.9 3.0 %collective-permute-start.4 = (bf16[516,512]{1,0:T(8,128)(2,1)S(1)}, bf16[516,512]{1,0:T(8,128)(2,1)S(1)}, u32[]{:S(2)}, u32[]{:S(2)}) collective-permute-start(bf16[516,512]{1,0:T(8,128)(2,1)S(1)} %get-tuple-element.52), channel_id=1, source_target_pairs={{0,6},{1,7},{2,0},{3,1},{4,2},{5,3},{6,4},{7,5},{8,14},{9,15},{10,... | collective-permute-start | bytes 1585160 | tf_op jit(solution)/shard_map/ppermute | solution.py:42
  23.9 1.5 collective-permute-start.3
  25.4 4.9 %fusion = f32[3,512,516]{1,2,0:T(8,128)S(1)} fusion(bf16[3,512,512]{2,1,0:T(8,128)(2,1)S(1)} %get-tuple-element.10, bf16[3,512,512]{2,1,0:T(8,128)(2,1)S(1)} %get-tuple-element.11, bf16[3,512,512]{2,1,0:T(8,128)(2,1)S(1)} %copy-done.2, bf16[3,512,512]{2,1,0:T(8,128)(2,1)S(1)} %copy-done.3, bf16[516,512]{1,0:T(8,128)(2,1)} %collective-permute-done.2, ...), kind=kOutput, calls=%fused_computation | convolution fusion | flops 3282124800 | bytes 11575296 | tf_op jit(solution)/shard_map/tn,cnf->ctf/dot_general | solution.py:175
  30.3 8.1 %collective-permute-done.5 = bf16[516,512]{1,0:T(8,128)(2,1)S(1)} collective-permute-done((bf16[516,512]{1,0:T(8,128)(2,1)S(1)}, bf16[516,512]{1,0:T(8,128)(2,1)S(1)}, u32[]{:S(2)}, u32[]{:S(2)}) %collective-permute-start.5) | collective-permute-done | bytes 528416 | tf_op jit(solution)/shard_map/ppermute | solution.py:42
  38.5 3.3 %collective-permute-start.7 = (bf16[516,128]{1,0:T(8,128)(2,1)S(1)}, bf16[516,128]{1,0:T(8,128)(2,1)S(1)}, u32[]{:S(2)}, u32[]{:S(2)}) collective-permute-start(bf16[516,128]{1,0:T(8,128)(2,1)S(1)} %slice.319), channel_id=1, source_target_pairs={{0,6},{1,7},{2,0},{3,1},{4,2},{5,3},{6,4},{7,5},{8,14},{9,15},{10,... | collective-permute-start | bytes 396296 | tf_op jit(solution)/shard_map/ppermute | solution.py:42
  41.9 0.8 collective-permute-start.6
  42.8 2.8 %fusion.8 = f32[3,512,516]{1,2,0:T(8,128)S(1)} fusion(bf16[3,512,512]{2,1,0:T(8,128)(2,1)S(1)} %get-tuple-element.14, bf16[3,512,512]{2,1,0:T(8,128)(2,1)S(1)} %get-tuple-element.9, bf16[3,512,512]{2,1,0:T(8,128)(2,1)S(1)} %get-tuple-element.8, bf16[516,1536]{1,0:T(8,128)(2,1)S(1)} %slice_dynamic-update-slice_fusion), kind=kOutput, calls=%fused_computation.8 | convolution fusion | flops 2448949248 | bytes 9474048 | tf_op jit(solution)/shard_map/tn,cnf->ctf/dot_general | solution.py:175
  45.6 3.0 %collective-permute-done.6 = bf16[516,256]{1,0:T(8,128)(2,1)S(1)} collective-permute-done((bf16[516,256]{1,0:T(8,128)(2,1)S(1)}, bf16[516,256]{1,0:T(8,128)(2,1)S(1)}, u32[]{:S(2)}, u32[]{:S(2)}) %collective-permute-start.6) | collective-permute-done | bytes 264224 | tf_op jit(solution)/shard_map/ppermute | solution.py:42
  48.6 2.7 %add_bitcast_fusion.proj_ref = f32[3,516,512]{2,1,0:T(8,128)S(1)} fusion(f32[3,512,516]{1,2,0:T(8,128)S(1)} %fusion, f32[3,512,516]{1,2,0:T(8,128)S(1)} %fusion.8, bf16[3,4096,512]{2,1,0:T(8,128)(2,1)} %param.10, s32[]{:T(128)S(6)} %select_n.128, bf16[516,128]{1,0:T(8,128)(2,1)S(1)} %collective-permute-done.8, ...), kind=kOutput, calls=%fused_computation.20 | convolution fusion | flops 814768128 | bytes 11612164 | tf_op jit(solution)/shard_map/tn,cnf->ctf/dot_general | solution.py:175
  52.3 1.0 fusion.101
  53.3 2.1 %collective-permute-done.9 = f32[2,516]{1,0:T(2,128)S(1)} collective-permute-done((f32[2,516]{1,0:T(2,128)S(1)}, f32[2,516]{1,0:T(2,128)S(1)}, u32[]{:S(2)}, u32[]{:S(2)}) %collective-permute-start.9) | collective-permute-done | bytes 4160 | tf_op jit(solution)/shard_map/ppermute | solution.py:82
  55.5 1.0 pad_maximum_fusion.12
  56.5 2.6 %collective-permute-done.10 = f32[2,516]{1,0:T(2,128)S(1)} collective-permute-done((f32[2,516]{1,0:T(2,128)S(1)}, f32[2,516]{1,0:T(2,128)S(1)}, u32[]{:S(2)}, u32[]{:S(2)}) %collective-permute-start.10) | collective-permute-done | bytes 4160 | tf_op jit(solution)/shard_map/ppermute | solution.py:82
  59.8 4.5 %collective-permute-done.11 = f32[2,516]{1,0:T(2,128)S(1)} collective-permute-done((f32[2,516]{1,0:T(2,128)S(1)}, f32[2,516]{1,0:T(2,128)S(1)}, u32[]{:S(2)}, u32[]{:S(2)}) %collective-permute-start.11) | collective-permute-done | bytes 4160 | tf_op jit(solution)/shard_map/ppermute | solution.py:82
  64.3 1.1 copy.10.square_ref
  65.4 4.1 %shard_map.95 = (bf16[16,3,128,128]{3,2,1,0:T(8,128)(2,1)}, f32[3,4,512]{2,1,0:T(4,128)}) custom-call(f32[3,516,512]{2,1,0:T(8,128)} %copy-done, f32[2,516,1]{2,1,0:T(8,128)} %copy.10.square_ref, f32[2,1,512]{2,1,0:T(1,128)} %broadcast_in_dim.65.gain_ref, f32[516,128]{1,0:T(8,128)} %get-tuple-element.71.cos_ref, f32[516,128]{1,0:T(8,128)} %get-tuple-element.72.sin_ref), custom_call_target="tpu_custom_call" | custom-call | tf_op jit(solution)/shard_map/pallas_call | solution.py:107
  69.5 7.7 %all-to-all-start = ((bf16[16,3,128,128]{3,2,1,0:T(8,128)(2,1)}), bf16[16,3,128,128]{3,2,1,0:T(8,128)(2,1)S(1)}, u32[]{:S(2)}, u32[]{:S(2)}) async-start(bf16[16,3,128,128]{3,2,1,0:T(8,128)(2,1)} %get-tuple-element.4), calls=%async_computation | async-start | bytes 3145728 | tf_op jit(solution)/shard_map/all_to_all | solution.py:204
  77.8 1.2 iota_compare_fusion.7
  79.0 1.2 iota_compare_fusion.6
  80.2 1.2 iota_compare_fusion.4
  82.0 1.2 iota_compare_fusion.5
  85.7 11.6 %all-to-all-done = bf16[16,3,128,128]{3,2,1,0:T(8,128)(2,1)S(1)} async-done(((bf16[16,3,128,128]{3,2,1,0:T(8,128)(2,1)}), bf16[16,3,128,128]{3,2,1,0:T(8,128)(2,1)S(1)}, u32[]{:S(2)}, u32[]{:S(2)}) %all-to-all-start) | async-done | bytes 1572896 | tf_op jit(solution)/shard_map/all_to_all | solution.py:204
  97.6 1.3 fusion.102
  99.6 1.9 fusion.105
  101.5 0.9 fusion.128
  102.4 0.8 fusion.130
  103.2 0.9 fusion.129
  104.8 2.3 %fusion.135 = (f32[512]{0:T(512)S(1)}, f32[512,2048]{1,0:T(8,128)S(1)}) fusion(bf16[512,128]{1,0:T(8,128)(2,1)} %bitcast.117, bf16[2048,128]{1,0:T(8,128)(2,1)S(1)} %bitcast.106, pred[2048]{0:T(1024)(128)(4,1)} %iota_compare_fusion.4, s32[512]{0:T(512)} %iota_add_fusion), kind=kOutput, calls=%fused_computation.214 | convolution fusion | flops 273677824 | bytes 4855808 | tf_op jit(solution)/shard_map/dot_general | solution.py:123
  107.1 1.5 fusion.17
  108.6 1.3 fusion.74
  110.0 1.1 fusion.136
  111.1 1.2 fusion.19
  112.3 1.0 fusion.68
  114.2 0.9 fusion.53
  117.4 0.8 pad_maximum_fusion.2
  118.3 8.0 %all-to-all-start.1 = ((bf16[16,136,128]{2,1,0:T(8,128)(2,1)}), bf16[16,136,128]{2,1,0:T(8,128)(2,1)S(1)}, u32[]{:S(2)}, u32[]{:S(2)}) async-start(bf16[16,136,128]{2,1,0:T(8,128)(2,1)} %pad_maximum_fusion.2), calls=%async_computation.1 | async-start | bytes 1114112 | tf_op jit(solution)/shard_map/all_to_all | solution.py:219
  126.3 3.3 %constant_dynamic-slice_fusion.6 = (bf16[512,512]{1,0:T(8,128)(2,1)S(1)}, bf16[512,512]{1,0:T(8,128)(2,1)S(1)}, bf16[512,512]{1,0:T(8,128)(2,1)S(1)}, bf16[512,5...) fusion(bf16[512,4096]{1,0:T(8,128)(2,1)} %param.11, ...), kind=kLoop, calls=%fused_computation.160 | loop fusion | bytes 7340060 | tf_op jit(solution)/shard_map/dynamic_slice | solution.py:167
  129.6 5.7 %all-to-all-done.1 = bf16[16,136,128]{2,1,0:T(8,128)(2,1)S(1)} async-done(((bf16[16,136,128]{2,1,0:T(8,128)(2,1)}), bf16[16,136,128]{2,1,0:T(8,128)(2,1)S(1)}, u32[]{:S(2)}, u32[]{:S(2)}) %all-to-all-start.1) | async-done | bytes 557088 | tf_op jit(solution)/shard_map/all_to_all | solution.py:219
  135.9 1.5 convolution_convert_fusion
  137.5 3.2 %collective-permute-start.15 = (bf16[516,128]{1,0:T(8,128)(2,1)S(1)}, bf16[516,128]{1,0:T(8,128)(2,1)S(1)}, u32[]{:S(2)}, u32[]{:S(2)}) collective-permute-start(bf16[516,128]{1,0:T(8,128)(2,1)S(1)} %get-tuple-element.46), channel_id=1, source_target_pairs={{0,6},{1,7},{2,0},{3,1},{4,2},{5,3},{6,4},{7,5},{8,14},{9,15},{10,... | collective-permute-start | bytes 396296 | tf_op jit(solution)/shard_map/ppermute | solution.py:62
  140.7 1.0 fusion.139
  142.0 2.1 %collective-permute-start.18 = (bf16[516,512]{1,0:T(8,128)(2,1)S(1)}, bf16[516,512]{1,0:T(8,128)(2,1)S(1)}, u32[]{:S(2)}, u32[]{:S(2)}) collective-permute-start(bf16[516,512]{1,0:T(8,128)(2,1)S(1)} %pad_maximum_fusion.8), channel_id=1, source_target_pairs={{0,1},{1,0},{2,3},{3,2},{4,5},{5,4},{6,7},{7,6},{8,9},{9,8},{10,11... | collective-permute-start | bytes 1585160 | tf_op jit(solution)/shard_map/ppermute | solution.py:62
  144.1 0.8 collective-permute-done.12
  145.1 3.0 %collective-permute-start.16 = (bf16[516,512]{1,0:T(8,128)(2,1)S(1)}, bf16[516,512]{1,0:T(8,128)(2,1)S(1)}, u32[]{:S(2)}, u32[]{:S(2)}) collective-permute-start(bf16[516,512]{1,0:T(8,128)(2,1)S(1)} %fusion.88), channel_id=1, source_target_pairs={{0,6},{1,7},{2,0},{3,1},{4,2},{5,3},{6,4},{7,5},{8,14},{9,15},{10,... | collective-permute-start | bytes 1585160 | tf_op jit(solution)/shard_map/ppermute | solution.py:62
  148.1 3.1 %collective-permute-done.13 = bf16[516,256]{1,0:T(8,128)(2,1)S(1)} collective-permute-done((bf16[516,256]{1,0:T(8,128)(2,1)S(1)}, bf16[516,256]{1,0:T(8,128)(2,1)S(1)}, u32[]{:S(2)}, u32[]{:S(2)}) %collective-permute-start.13) | collective-permute-done | bytes 264224 | tf_op jit(solution)/shard_map/ppermute | solution.py:62
  151.5 1.3 fusion.140
  152.8 9.1 %collective-permute-done.18 = bf16[516,512]{1,0:T(8,128)(2,1)S(1)} collective-permute-done((bf16[516,512]{1,0:T(8,128)(2,1)S(1)}, bf16[516,512]{1,0:T(8,128)(2,1)S(1)}, u32[]{:S(2)}, u32[]{:S(2)}) %collective-permute-start.18) | collective-permute-done | bytes 528416 | tf_op jit(solution)/shard_map/ppermute | solution.py:62
  162.2 3.1 %collective-permute-done.14 = bf16[516,512]{1,0:T(8,128)(2,1)S(1)} collective-permute-done((bf16[516,512]{1,0:T(8,128)(2,1)S(1)}, bf16[516,512]{1,0:T(8,128)(2,1)S(1)}, u32[]{:S(2)}, u32[]{:S(2)}) %collective-permute-start.14) | collective-permute-done | bytes 528416 | tf_op jit(solution)/shard_map/ppermute | solution.py:62
  166.2 2.1 %collective-permute-start.19 = (bf16[516,512]{1,0:T(8,128)(2,1)S(1)}, bf16[516,512]{1,0:T(8,128)(2,1)S(1)}, u32[]{:S(2)}, u32[]{:S(2)}) collective-permute-start(bf16[516,512]{1,0:T(8,128)(2,1)S(1)} %pad_maximum_fusion.9), channel_id=1, source_target_pairs={{0,2},{1,3},{2,4},{3,5},{4,6},{5,7},{6,0},{7,1},{8,10},{9,11},{10,... | collective-permute-start | bytes 1585160 | tf_op jit(solution)/shard_map/ppermute | solution.py:62
  169.0 8.9 %collective-permute-done.20 = bf16[516,512]{1,0:T(8,128)(2,1)S(1)} collective-permute-done((bf16[516,512]{1,0:T(8,128)(2,1)S(1)}, bf16[516,512]{1,0:T(8,128)(2,1)S(1)}, u32[]{:S(2)}, u32[]{:S(2)}) %collective-permute-start.20) | collective-permute-done | bytes 528416 | tf_op jit(solution)/shard_map/ppermute | solution.py:62
  177.9 1.3 collective-permute-done.19
  180.0 1.3 collective-permute-start.21
  181.2 2.4 %collective-permute-done.21 = f32[516]{0:T(1024)S(1)} collective-permute-done((f32[516]{0:T(1024)S(1)}, f32[516]{0:T(1024)S(1)}, u32[]{:S(2)}, u32[]{:S(2)}) %collective-permute-start.21) | collective-permute-done | bytes 2096 | tf_op jit(solution)/shard_map/ppermute | solution.py:82
  184.0 3.3 %collective-permute-done.22 = f32[516]{0:T(1024)S(1)} collective-permute-done((f32[516]{0:T(1024)S(1)}, f32[516]{0:T(1024)S(1)}, u32[]{:S(2)}, u32[]{:S(2)}) %collective-permute-start.22) | collective-permute-done | bytes 2096 | tf_op jit(solution)/shard_map/ppermute | solution.py:82
  187.3 0.9 collective-permute-start.23
  188.2 4.2 %collective-permute-done.23 = f32[516]{0:T(1024)S(1)} collective-permute-done((f32[516]{0:T(1024)S(1)}, f32[516]{0:T(1024)S(1)}, u32[]{:S(2)}, u32[]{:S(2)}) %collective-permute-start.23) | collective-permute-done | bytes 2096 | tf_op jit(solution)/shard_map/ppermute | solution.py:82
  192.8 0.8 slice.361
  (150 shorter events, 14.6 us)
Async XLA Ops:
  1.7 17.9 %collective-permute-start.2 = (bf16[516,512]{1,0:T(8,128)(2,1)S(1)}, bf16[516,512]{1,0:T(8,128)(2,1)}, u32[]{:S(2)}, u32[]{:S(2)}) collective-permute-start(bf16[516,512]{1,0:T(8,128)(2,1)S(1)} %pad_maximum_fusion.4), channel_id=1, source_target_pairs={{0,6},{1,7},{2,0},{3,1},{4,2},{5,3},{6,4},{7,5},{8,14},{9,15},{10,... | collective-permute-start | bytes 1585160 | tf_op jit(solution)/shard_map/ppermute | solution.py:42
  4.8 14.8 %collective-permute-start.1 = (bf16[516,512]{1,0:T(8,128)(2,1)S(1)}, bf16[516,512]{1,0:T(8,128)(2,1)S(1)}, u32[]{:S(2)}, u32[]{:S(2)}) collective-permute-start(bf16[516,512]{1,0:T(8,128)(2,1)S(1)} %pad_maximum_fusion.4), channel_id=1, source_target_pairs={{0,2},{1,3},{2,4},{3,5},{4,6},{5,7},{6,0},{7,1},{8,10},{9,11},{10,... | collective-permute-start | bytes 1585160 | tf_op jit(solution)/shard_map/ppermute | solution.py:42
  4.8 13.7 %collective-permute-start = (bf16[516,512]{1,0:T(8,128)(2,1)S(1)}, bf16[516,512]{1,0:T(8,128)(2,1)}, u32[]{:S(2)}, u32[]{:S(2)}) collective-permute-start(bf16[516,512]{1,0:T(8,128)(2,1)S(1)} %pad_maximum_fusion.4), channel_id=1, source_target_pairs={{0,1},{1,0},{2,3},{3,2},{4,5},{5,4},{6,7},{7,6},{8,9},{9,8},{10,11... | collective-permute-start | bytes 1585160 | tf_op jit(solution)/shard_map/ppermute | solution.py:42
  19.5 5.9 %copy-start.1 = (bf16[4,128,512]{2,1,0:T(8,128)(2,1)S(1)}, bf16[4,128,512]{2,1,0:T(8,128)(2,1)}, u32[]{:S(2)}) copy-start(bf16[4,128,512]{2,1,0:T(8,128)(2,1)} %param.8) | copy-start | bytes 1572868
  19.5 5.9 %copy-start.2 = (bf16[3,512,512]{2,1,0:T(8,128)(2,1)S(1)}, bf16[3,512,512]{2,1,0:T(8,128)(2,1)}, u32[]{:S(2)}) copy-start(bf16[3,512,512]{2,1,0:T(8,128)(2,1)} %get-tuple-element.12) | copy-start | bytes 4718596
  19.5 5.9 %copy-start.3 = (bf16[3,512,512]{2,1,0:T(8,128)(2,1)S(1)}, bf16[3,512,512]{2,1,0:T(8,128)(2,1)}, u32[]{:S(2)}) copy-start(bf16[3,512,512]{2,1,0:T(8,128)(2,1)} %get-tuple-element.13) | copy-start | bytes 4718596
  19.5 5.9 %copy-start.16 = (bf16[4,512]{1,0:T(4,128)(2,1)S(1)}, bf16[4,512]{1,0:T(4,128)(2,1)}, u32[]{:S(2)}) copy-start(bf16[4,512]{1,0:T(4,128)(2,1)} %param.9) | copy-start | bytes 12292
  20.9 17.6 %collective-permute-start.4 = (bf16[516,512]{1,0:T(8,128)(2,1)S(1)}, bf16[516,512]{1,0:T(8,128)(2,1)S(1)}, u32[]{:S(2)}, u32[]{:S(2)}) collective-permute-start(bf16[516,512]{1,0:T(8,128)(2,1)S(1)} %get-tuple-element.52), channel_id=1, source_target_pairs={{0,6},{1,7},{2,0},{3,1},{4,2},{5,3},{6,4},{7,5},{8,14},{9,15},{10,... | collective-permute-start | bytes 1585160 | tf_op jit(solution)/shard_map/ppermute | solution.py:42
  23.9 17.9 %collective-permute-start.3 = (bf16[516,512]{1,0:T(8,128)(2,1)S(1)}, bf16[516,512]{1,0:T(8,128)(2,1)S(1)}, u32[]{:S(2)}, u32[]{:S(2)}) collective-permute-start(bf16[516,512]{1,0:T(8,128)(2,1)S(1)} %get-tuple-element.53), channel_id=1, source_target_pairs={{0,1},{1,0},{2,3},{3,2},{4,5},{5,4},{6,7},{7,6},{8,9},{9,8},{10,11... | collective-permute-start | bytes 1585160 | tf_op jit(solution)/shard_map/ppermute | solution.py:42
  25.4 13.0 %collective-permute-start.5 = (bf16[516,512]{1,0:T(8,128)(2,1)S(1)}, bf16[516,512]{1,0:T(8,128)(2,1)S(1)}, u32[]{:S(2)}, u32[]{:S(2)}) collective-permute-start(bf16[516,512]{1,0:T(8,128)(2,1)S(1)} %get-tuple-element.51), channel_id=1, source_target_pairs={{0,2},{1,3},{2,4},{3,5},{4,6},{5,7},{6,0},{7,1},{8,10},{9,11},{10,... | collective-permute-start | bytes 1585160 | tf_op jit(solution)/shard_map/ppermute | solution.py:42
  38.4 7.2 %collective-permute-start.8 = (bf16[516,128]{1,0:T(8,128)(2,1)S(1)}, bf16[516,128]{1,0:T(8,128)(2,1)S(1)}, u32[]{:S(2)}, u32[]{:S(2)}) collective-permute-start(bf16[516,128]{1,0:T(8,128)(2,1)S(1)} %slice.320), channel_id=1, source_target_pairs={{0,2},{1,3},{2,4},{3,5},{4,6},{5,7},{6,0},{7,1},{8,10},{9,11},{10,... | collective-permute-start | bytes 396296 | tf_op jit(solution)/shard_map/ppermute | solution.py:42
  38.5 7.1 %collective-permute-start.7 = (bf16[516,128]{1,0:T(8,128)(2,1)S(1)}, bf16[516,128]{1,0:T(8,128)(2,1)S(1)}, u32[]{:S(2)}, u32[]{:S(2)}) collective-permute-start(bf16[516,128]{1,0:T(8,128)(2,1)S(1)} %slice.319), channel_id=1, source_target_pairs={{0,6},{1,7},{2,0},{3,1},{4,2},{5,3},{6,4},{7,5},{8,14},{9,15},{10,... | collective-permute-start | bytes 396296 | tf_op jit(solution)/shard_map/ppermute | solution.py:42
  41.9 6.7 %collective-permute-start.6 = (bf16[516,256]{1,0:T(8,128)(2,1)S(1)}, bf16[516,256]{1,0:T(8,128)(2,1)S(1)}, u32[]{:S(2)}, u32[]{:S(2)}) collective-permute-start(bf16[516,256]{1,0:T(8,128)(2,1)S(1)} %get-tuple-element.47), channel_id=1, source_target_pairs={{0,1},{1,0},{2,3},{3,2},{4,5},{5,4},{6,7},{7,6},{8,9},{9,8},{10,11... | collective-permute-start | bytes 792584 | tf_op jit(solution)/shard_map/ppermute | solution.py:42
  51.3 5.2 %copy-start = (f32[3,516,512]{2,1,0:T(8,128)}, f32[3,516,512]{2,1,0:T(8,128)S(1)}, u32[]{:S(2)}) copy-start(f32[3,516,512]{2,1,0:T(8,128)S(1)} %add_bitcast_fusion.proj_ref) | copy-start | bytes 9510916
  51.3 7.8 %copy-start.24 = (f32[512]{0:T(512)S(1)}, f32[512]{0:T(512)}, u32[]{:S(2)}) copy-start(f32[512]{0:T(512)} %param.13) | copy-start | bytes 6148
  51.4 7.8 %copy-start.25 = (f32[512]{0:T(512)S(1)}, f32[512]{0:T(512)}, u32[]{:S(2)}) copy-start(f32[512]{0:T(512)} %param.12) | copy-start | bytes 6148
  51.7 3.7 %collective-permute-start.9 = (f32[2,516]{1,0:T(2,128)S(1)}, f32[2,516]{1,0:T(2,128)S(1)}, u32[]{:S(2)}, u32[]{:S(2)}) collective-permute-start(f32[2,516]{1,0:T(2,128)S(1)} %pad_maximum_fusion.14), channel_id=1, source_target_pairs={{0,1},{1,0},{2,3},{3,2},{4,5},{5,4},{6,7},{7,6},{8,9},{9,8},{10,11... | collective-permute-start | bytes 12392 | tf_op jit(solution)/shard_map/ppermute | solution.py:82
  55.4 3.7 %collective-permute-start.10 = (f32[2,516]{1,0:T(2,128)S(1)}, f32[2,516]{1,0:T(2,128)S(1)}, u32[]{:S(2)}, u32[]{:S(2)}) collective-permute-start(f32[2,516]{1,0:T(2,128)S(1)} %fusion.125), channel_id=1, source_target_pairs={{0,2},{1,3},{2,0},{3,1},{4,6},{5,7},{6,4},{7,5},{8,10},{9,11},{10,... | collective-permute-start | bytes 12392 | tf_op jit(solution)/shard_map/ppermute | solution.py:82
  59.1 5.2 %collective-permute-start.11 = (f32[2,516]{1,0:T(2,128)S(1)}, f32[2,516]{1,0:T(2,128)S(1)}, u32[]{:S(2)}, u32[]{:S(2)}) collective-permute-start(f32[2,516]{1,0:T(2,128)S(1)} %fusion.159), channel_id=1, source_target_pairs={{0,4},{1,5},{2,6},{3,7},{4,0},{5,1},{6,2},{7,3},{8,12},{9,13},{10,... | collective-permute-start | bytes 12392 | tf_op jit(solution)/shard_map/ppermute | solution.py:82
  69.5 7.7 %copy-start.28 = (s32[4]{0:T(128)S(1)}, s32[4]{0:T(128)}, u32[]{:S(2)}) copy-start(s32[4]{0:T(128)} %param.15) | copy-start | bytes 52
  69.5 14.9 %copy-start.15 = (f32[3,4,512]{2,1,0:T(4,128)S(1)}, f32[3,4,512]{2,1,0:T(4,128)}, u32[]{:S(2)}) copy-start(f32[3,4,512]{2,1,0:T(4,128)} %get-tuple-element.5) | copy-start | bytes 73732
  69.5 27.8 %all-to-all-start = ((bf16[16,3,128,128]{3,2,1,0:T(8,128)(2,1)}), bf16[16,3,128,128]{3,2,1,0:T(8,128)(2,1)S(1)}, u32[]{:S(2)}, u32[]{:S(2)}) async-start(bf16[16,3,128,128]{3,2,1,0:T(8,128)(2,1)} %get-tuple-element.4), calls=%async_computation | async-start | bytes 3145728 | tf_op jit(solution)/shard_map/all_to_all | solution.py:204
  101.5 2.6 %copy-start.17 = (bf16[2048]{0:T(1024)(128)(2,1)S(1)}, bf16[2048]{0:T(1024)(128)(2,1)}, u32[]{:S(2)}) copy-start(bf16[2048]{0:T(1024)(128)(2,1)} %get-tuple-element.55) | copy-start | bytes 12292
  104.8 2.3 %copy-start.19 = (pred[2048]{0:T(1024)(128)(4,1)S(1)}, pred[2048]{0:T(1024)(128)(4,1)}, u32[]{:S(2)}) copy-start(pred[2048]{0:T(1024)(128)(4,1)} %iota_compare_fusion.4) | copy-start | bytes 6148
  104.8 2.3 %copy-start.22 = (s32[512]{0:T(512)S(1)}, s32[512]{0:T(512)}, u32[]{:S(2)}) copy-start(s32[512]{0:T(512)} %iota_add_fusion) | copy-start | bytes 6148
  108.6 1.4 copy-start.7
  108.6 1.4 copy-start.14
  108.6 1.4 copy-start.18
  108.6 1.4 copy-start.21
  112.2 1.1 copy-start.9
  112.3 1.1 copy-start.13
  112.3 1.1 copy-start.20
  112.3 1.1 copy-start.26
  113.4 1.6 copy-start.8
  115.0 0.9 copy-start.11
  115.0 1.0 copy-start.12
  115.0 1.0 copy-start.27
  115.8 0.9 copy-start.10
  118.3 17.1 %all-to-all-start.1 = ((bf16[16,136,128]{2,1,0:T(8,128)(2,1)}), bf16[16,136,128]{2,1,0:T(8,128)(2,1)S(1)}, u32[]{:S(2)}, u32[]{:S(2)}) async-start(bf16[16,136,128]{2,1,0:T(8,128)(2,1)} %pad_maximum_fusion.2), calls=%async_computation.1 | async-start | bytes 1114112 | tf_op jit(solution)/shard_map/all_to_all | solution.py:219
  137.4 7.5 %collective-permute-start.12 = (bf16[516,128]{1,0:T(8,128)(2,1)S(1)}, bf16[516,128]{1,0:T(8,128)(2,1)S(1)}, u32[]{:S(2)}, u32[]{:S(2)}) collective-permute-start(bf16[516,128]{1,0:T(8,128)(2,1)S(1)} %get-tuple-element.45), channel_id=1, source_target_pairs={{0,2},{1,3},{2,4},{3,5},{4,6},{5,7},{6,0},{7,1},{8,10},{9,11},{10,... | collective-permute-start | bytes 396296 | tf_op jit(solution)/shard_map/ppermute | solution.py:62
  137.5 7.4 %collective-permute-start.15 = (bf16[516,128]{1,0:T(8,128)(2,1)S(1)}, bf16[516,128]{1,0:T(8,128)(2,1)S(1)}, u32[]{:S(2)}, u32[]{:S(2)}) collective-permute-start(bf16[516,128]{1,0:T(8,128)(2,1)S(1)} %get-tuple-element.46), channel_id=1, source_target_pairs={{0,6},{1,7},{2,0},{3,1},{4,2},{5,3},{6,4},{7,5},{8,14},{9,15},{10,... | collective-permute-start | bytes 396296 | tf_op jit(solution)/shard_map/ppermute | solution.py:62
  141.9 9.3 %collective-permute-start.13 = (bf16[516,256]{1,0:T(8,128)(2,1)S(1)}, bf16[516,256]{1,0:T(8,128)(2,1)S(1)}, u32[]{:S(2)}, u32[]{:S(2)}) collective-permute-start(bf16[516,256]{1,0:T(8,128)(2,1)S(1)} %slice.344), channel_id=1, source_target_pairs={{0,1},{1,0},{2,3},{3,2},{4,5},{5,4},{6,7},{7,6},{8,9},{9,8},{10,11... | collective-permute-start | bytes 792584 | tf_op jit(solution)/shard_map/ppermute | solution.py:62
  142.0 19.9 %collective-permute-start.18 = (bf16[516,512]{1,0:T(8,128)(2,1)S(1)}, bf16[516,512]{1,0:T(8,128)(2,1)S(1)}, u32[]{:S(2)}, u32[]{:S(2)}) collective-permute-start(bf16[516,512]{1,0:T(8,128)(2,1)S(1)} %pad_maximum_fusion.8), channel_id=1, source_target_pairs={{0,1},{1,0},{2,3},{3,2},{4,5},{5,4},{6,7},{7,6},{8,9},{9,8},{10,11... | collective-permute-start | bytes 1585160 | tf_op jit(solution)/shard_map/ppermute | solution.py:62
  144.9 6.5 %copy-start.4 = (bf16[512,512]{1,0:T(8,128)(2,1)S(1)}, bf16[512,512]{1,0:T(8,128)(2,1)}, u32[]{:S(2)}) copy-start(bf16[512,512]{1,0:T(8,128)(2,1)} %get-tuple-element.22) | copy-start | bytes 1572868
  144.9 6.5 %copy-start.5 = (bf16[512,512]{1,0:T(8,128)(2,1)S(1)}, bf16[512,512]{1,0:T(8,128)(2,1)}, u32[]{:S(2)}) copy-start(bf16[512,512]{1,0:T(8,128)(2,1)} %get-tuple-element.23) | copy-start | bytes 1572868
  144.9 6.5 %copy-start.6 = (bf16[512,512]{1,0:T(8,128)(2,1)S(1)}, bf16[512,512]{1,0:T(8,128)(2,1)}, u32[]{:S(2)}) copy-start(bf16[512,512]{1,0:T(8,128)(2,1)} %get-tuple-element.24) | copy-start | bytes 1572868
  145.1 17.0 %collective-permute-start.16 = (bf16[516,512]{1,0:T(8,128)(2,1)S(1)}, bf16[516,512]{1,0:T(8,128)(2,1)S(1)}, u32[]{:S(2)}, u32[]{:S(2)}) collective-permute-start(bf16[516,512]{1,0:T(8,128)(2,1)S(1)} %fusion.88), channel_id=1, source_target_pairs={{0,6},{1,7},{2,0},{3,1},{4,2},{5,3},{6,4},{7,5},{8,14},{9,15},{10,... | collective-permute-start | bytes 1585160 | tf_op jit(solution)/shard_map/ppermute | solution.py:62
  151.4 14.0 %collective-permute-start.14 = (bf16[516,512]{1,0:T(8,128)(2,1)S(1)}, bf16[516,512]{1,0:T(8,128)(2,1)S(1)}, u32[]{:S(2)}, u32[]{:S(2)}) collective-permute-start(bf16[516,512]{1,0:T(8,128)(2,1)S(1)} %pad_maximum_fusion.6), channel_id=1, source_target_pairs={{0,2},{1,3},{2,4},{3,5},{4,6},{5,7},{6,0},{7,1},{8,10},{9,11},{10,... | collective-permute-start | bytes 1585160 | tf_op jit(solution)/shard_map/ppermute | solution.py:62
  166.0 11.8 %collective-permute-start.20 = (bf16[516,512]{1,0:T(8,128)(2,1)S(1)}, bf16[516,512]{1,0:T(8,128)(2,1)S(1)}, u32[]{:S(2)}, u32[]{:S(2)}) collective-permute-start(bf16[516,512]{1,0:T(8,128)(2,1)S(1)} %pad_maximum_fusion.10), channel_id=1, source_target_pairs={{0,6},{1,7},{2,0},{3,1},{4,2},{5,3},{6,4},{7,5},{8,14},{9,15},{10,... | collective-permute-start | bytes 1585160 | tf_op jit(solution)/shard_map/ppermute | solution.py:62
  166.2 26.2 %copy-start.23 = (f32[512]{0:T(512)S(1)}, f32[512]{0:T(512)}, u32[]{:S(2)}) copy-start(f32[512]{0:T(512)} %param.14) | copy-start | bytes 6148
  166.2 13.0 %collective-permute-start.19 = (bf16[516,512]{1,0:T(8,128)(2,1)S(1)}, bf16[516,512]{1,0:T(8,128)(2,1)S(1)}, u32[]{:S(2)}, u32[]{:S(2)}) collective-permute-start(bf16[516,512]{1,0:T(8,128)(2,1)S(1)} %pad_maximum_fusion.9), channel_id=1, source_target_pairs={{0,2},{1,3},{2,4},{3,5},{4,6},{5,7},{6,0},{7,1},{8,10},{9,11},{10,... | collective-permute-start | bytes 1585160 | tf_op jit(solution)/shard_map/ppermute | solution.py:62
  168.3 11.3 %collective-permute-start.17 = (bf16[516,512]{1,0:T(8,128)(2,1)S(1)}, bf16[516,512]{1,0:T(8,128)(2,1)S(1)}, u32[]{:S(2)}, u32[]{:S(2)}) collective-permute-start(bf16[516,512]{1,0:T(8,128)(2,1)S(1)} %pad_maximum_fusion.7), channel_id=1, source_target_pairs={{0,1},{1,0},{2,3},{3,2},{4,5},{5,4},{6,7},{7,6},{8,9},{9,8},{10,11... | collective-permute-start | bytes 1585160 | tf_op jit(solution)/shard_map/ppermute | solution.py:62
  180.0 3.7 %collective-permute-start.21 = (f32[516]{0:T(1024)S(1)}, f32[516]{0:T(1024)S(1)}, u32[]{:S(2)}, u32[]{:S(2)}) collective-permute-start(f32[516]{0:T(1024)S(1)} %multiply_reduce_fusion), channel_id=1, source_target_pairs={{0,1},{1,0},{2,3},{3,2},{4,5},{5,4},{6,7},{7,6},{8,9},{9,8},{10,11... | collective-permute-start | bytes 6200 | tf_op jit(solution)/shard_map/ppermute | solution.py:82
  183.7 3.6 %collective-permute-start.22 = (f32[516]{0:T(1024)S(1)}, f32[516]{0:T(1024)S(1)}, u32[]{:S(2)}, u32[]{:S(2)}) collective-permute-start(f32[516]{0:T(1024)S(1)} %add.274), channel_id=1, source_target_pairs={{0,2},{1,3},{2,0},{3,1},{4,6},{5,7},{6,4},{7,5},{8,10},{9,11},{10,... | collective-permute-start | bytes 6200 | tf_op jit(solution)/shard_map/ppermute | solution.py:82
  187.3 5.1 %collective-permute-start.23 = (f32[516]{0:T(1024)S(1)}, f32[516]{0:T(1024)S(1)}, u32[]{:S(2)}, u32[]{:S(2)}) collective-permute-start(f32[516]{0:T(1024)S(1)} %add.275), channel_id=1, source_target_pairs={{0,4},{1,5},{2,6},{3,7},{4,0},{5,1},{6,2},{7,3},{8,12},{9,13},{10,... | collective-permute-start | bytes 6200 | tf_op jit(solution)/shard_map/ppermute | solution.py:82
